TPU v7x, 512 devices: a whole 4x4x16 slice. The times are simulated.
512 devices in a mesh: clip: 16 (over y, z_hi), seq: 32 (over x, z_lo, core).
Axes of the slice: x: 4, y: 4, z: 16 (z_hi: 4, z_lo: 4; z = z_hi * 4 + z_lo), core: 2. Of those that a mesh axis runs over, the one named last changes fastest.
Arguments:
- frames_in: bfloat16 [512, 256, 1152], P(('clip', 'seq')), parts along dimension 0, may hold values from -6 to 6
- modulation: float32 [48, 1152], P('clip'), parts along dimension 0, may hold values from -3 to 3
- self_proj: bfloat16 [1152, 1728], P(None, 'seq'), may hold values from -0.1875 to 0.1875
- self_out: bfloat16 [576, 1152], P(None, 'seq'), may hold values from -0.25 to 0.25
- cross_query: bfloat16 [1152, 576], P(None, 'seq'), may hold values from -0.1875 to 0.1875
- cross_keyval: bfloat16 [1152, 1152], P(None, 'seq'), may hold values from -0.1875 to 0.1875
- cross_out: bfloat16 [576, 1152], P(None, 'seq'), may hold values from -0.25 to 0.25
- text_bank: bfloat16 [32, 256, 1152], P('seq'), may hold values from -6 to 6
- prompt_pick: int32 [16], P('clip'), parts along dimension 0, may hold values from 0 to 31
- text_lengths: int32 [32], replicated, may hold values from 32 to 256
Outputs:
- frames_out: bfloat16 [512, 256, 1152], P(('clip', 'seq')), parts along dimension 0
There are 16 independent parts, one for each index of `clip`. A program takes and returns all parts, laid end to end along the dimension named above; an argument that names none is the same for every part. Nothing has to cross between parts.
All inputs are finite; a program needn't handle non-finite values.
Results may differ from a plain program's by a relative error of at most 0.006.
Values may be sent and summed in bfloat16 or wider, within the bound.
No kernel may reach another device: no remote copies, remote signals or barrier semaphores. Data moves between devices by JAX's collectives and lax.ppermute only.
A program may use at most 64 MiB of HBM per device.

v0:
```python
import math

import jax
import jax.numpy as jnp
from jax import lax
from jax.sharding import PartitionSpec as P

HEAD_DIM = 72


EPS = 1e-06


def spread_2(block, axis, owner):
    block = jnp.where(lax.axis_index(axis) == owner, block, jnp.zeros_like(block))
    return lax.psum(block, axis)


def layer_norm(values):
    mean = jnp.mean(values, axis=-1, keepdims=True)
    centred = values - mean
    spread = jnp.mean(centred * centred, axis=-1, keepdims=True)
    return centred * lax.rsqrt(spread + EPS)


def head_norm(values, heads):
    shaped = values.reshape(values.shape[:-1] + (heads, values.shape[-1] // heads))
    power = jnp.mean(shaped * shaped, axis=-1, keepdims=True)
    return shaped * lax.rsqrt(power + EPS)


def temporal_attention(qkv, heads, attn, scale_q):
    frames, patches = (qkv.shape[0], qkv.shape[1])
    query = (head_norm(qkv[..., :attn].astype(jnp.float32), heads) * scale_q).astype(jnp.bfloat16)
    key = head_norm(qkv[..., attn : 2 * attn].astype(jnp.float32), heads).astype(jnp.bfloat16)
    value = qkv[..., 2 * attn :].reshape(frames, patches, heads, attn // heads)
    scores = jnp.einsum("fphd,gphd->phfg", query, key, preferred_element_type=jnp.float32)
    weights = jnp.exp(scores)
    total = jnp.sum(weights, axis=-1)
    probs = weights.astype(jnp.bfloat16)
    mixed = jnp.einsum("phfg,gphd->fphd", probs, value, preferred_element_type=jnp.float32)
    attended = mixed / jnp.transpose(total, (2, 0, 1))[..., None]
    return attended.astype(jnp.bfloat16).reshape(frames, patches, attn)


def per_device(
    frames_in,
    modulation,
    self_proj,
    self_out,
    cross_query,
    cross_keyval,
    cross_out,
    text_bank,
    prompt_pick,
    text_lengths,
):
    count = lax.axis_size("seq")
    frame_rows, pixels, width = frames_in.shape
    attn = self_out.shape[0]
    heads = attn // HEAD_DIM
    scale_q = 1.0 / math.sqrt(HEAD_DIM)
    pix_dev = pixels // count
    frames = frame_rows * count
    tokens = frames_in.astype(jnp.float32)
    normed = (layer_norm(tokens) * (1.0 + modulation[1]) + modulation[0]).astype(jnp.bfloat16)
    switched = lax.all_to_all(normed, "seq", split_axis=1, concat_axis=0, tiled=True)
    flat_pix = switched.reshape(-1, width)
    qkv = jnp.dot(
        flat_pix,
        lax.all_gather(self_proj, "seq", axis=1, tiled=True),
        preferred_element_type=jnp.float32,
    ).astype(jnp.bfloat16)
    qkv = qkv.reshape(frames, pix_dev, 3 * attn)
    out_self, query_weight, out_cross = (
        lax.all_gather(self_out, "seq", axis=1, tiled=True),
        lax.all_gather(cross_query, "seq", axis=1, tiled=True),
        lax.all_gather(cross_out, "seq", axis=1, tiled=True),
    )
    attended = temporal_attention(qkv, heads, attn, scale_q)
    returned = lax.all_to_all(attended, "seq", split_axis=0, concat_axis=1, tiled=True)
    self_term = jnp.dot(returned.reshape(-1, attn), out_self, preferred_element_type=jnp.float32)
    after_self = (tokens.reshape(-1, width) + modulation[2] * self_term).astype(jnp.bfloat16)
    pick = prompt_pick[0]
    memory = spread_2(text_bank[0], "seq", pick)
    own_columns = jnp.dot(memory, cross_keyval, preferred_element_type=jnp.float32).astype(
        jnp.bfloat16
    )
    keyval = lax.all_gather(own_columns, "seq", axis=1, tiled=True)
    text_len = keyval.shape[0]
    text_key = head_norm(keyval[:, :attn].astype(jnp.float32), heads).astype(jnp.bfloat16)
    text_value = keyval[:, attn:].reshape(text_len, heads, HEAD_DIM)
    slots = jnp.arange(text_lengths.shape[0], dtype=jnp.int32)
    length = jnp.sum(jnp.where(slots == pick, text_lengths, 0))
    live = jnp.arange(text_len, dtype=jnp.int32) < length
    text_query = jnp.dot(after_self, query_weight, preferred_element_type=jnp.float32)
    text_query = (head_norm(text_query, heads) * scale_q).astype(jnp.bfloat16)
    cross_scores = jnp.einsum(
        "thd,lhd->thl", text_query, text_key, preferred_element_type=jnp.float32
    )
    cross_weights = jnp.where(live, jnp.exp(cross_scores), 0.0)
    cross_total = jnp.sum(cross_weights, axis=-1)
    cross_probs = cross_weights.astype(jnp.bfloat16)
    cross_mix = jnp.einsum(
        "thl,lhd->thd", cross_probs, text_value, preferred_element_type=jnp.float32
    )
    crossed = (cross_mix / cross_total[..., None]).astype(jnp.bfloat16).reshape(-1, attn)
    cross_term = jnp.dot(crossed, out_cross, preferred_element_type=jnp.float32)
    frames_out = (after_self.astype(jnp.float32) + cross_term).astype(jnp.bfloat16)
    return frames_out.reshape(frame_rows, pixels, width)


def solution(mesh):
    placed = (
        P(("clip", "seq"), None, None),
        P("clip", None),
        P(None, "seq"),
        P(None, "seq"),
        P(None, "seq"),
        P(None, "seq"),
        P(None, "seq"),
        P("seq", None, None),
        P("clip"),
        P(),
    )
    return jax.shard_map(
        per_device,
        mesh=mesh,
        in_specs=placed,
        out_specs=P(("clip", "seq"), None, None),
        check_vma=False,
    )
```

profile of v0, /device:TPU:1, one launch (start us, length us, event | category | flops | bytes accessed | tf_op | source)
XLA Modules:
  0.0 582.2 jit_solution(11461628995922027875)
XLA Ops:
  6.5 0.7 all-gather.10.cloned.1.call-update
  8.0 0.9 select_bitcast_fusion
  8.9 0.7 all-gather.12.cloned.1.call-update
  11.0 0.9 copy.54
  12.5 4.3 reduce.8
  16.9 1.0 reshape.164
  17.9 10.4 %all-to-all-start = ((bf16[32,2,4608]{2,1,0:T(2,128)(2,1)}), bf16[32,2,4608]{2,1,0:T(2,128)(2,1)S(1)}, u32[]{:S(2)}, u32[]{:S(2)}) async-start(bf16[32,2,4608]{2,1,0:T(2,128)(2,1)} %reshape.164), calls=%async_computation | async-start | bytes 1179648 | tf_op jit(solution)/shard_map/all_to_all | solution.py:67
  29.6 20.2 %all-to-all-done = bf16[32,2,4608]{2,1,0:T(2,128)(2,1)S(1)} async-done(((bf16[32,2,4608]{2,1,0:T(2,128)(2,1)}), bf16[32,2,4608]{2,1,0:T(2,128)(2,1)S(1)}, u32[]{:S(2)}, u32[]{:S(2)}) %all-to-all-start) | async-done | bytes 589856 | tf_op jit(solution)/shard_map/all_to_all | solution.py:67
  50.2 37.1 %all-gather.10.cloned.1.call-done = bf16[32,54,1152]{2,1,0:T(8,128)(2,1)} async-done(((bf16[1,54,1152]{2,1,0:T(8,128)(2,1)}), bf16[32,54,1152]{2,1,0:T(8,128)(2,1)}) %all-gather.10.cloned.1.call-update) | async-done | bytes 3981328 | tf_op jit(solution)/shard_map/all_gather | solution.py:71
  87.3 5.0 reshape.150
  92.3 3.5 convolution_convert_fusion
  96.5 0.9 slice_convert_fusion.1
  97.8 1.0 multiply_reduce_fusion
  99.3 1.6 reshape.130
  101.3 0.7 multiply_convert_fusion
  102.0 0.9 fusion.35
  102.9 0.7 fusion.7
  103.9 1.1 reshape.135
  104.9 6.6 %all-to-all-start.1 = ((bf16[32,8,576]{2,1,0:T(8,128)(2,1)}), bf16[32,8,576]{2,1,0:T(8,128)(2,1)}, u32[]{:S(2)}, u32[]{:S(2)}) async-start(bf16[32,8,576]{2,1,0:T(8,128)(2,1)} %reshape.135), calls=%async_computation.1 | async-start | bytes 655360 | tf_op jit(solution)/shard_map/all_to_all | solution.py:81
  112.2 254.0 %all-reduce.2.cloned.1.call-done = bf16[256,1152]{1,0:T(8,128)(2,1)} async-done(((bf16[256,1152]{1,0:T(8,128)(2,1)}), bf16[256,1152]{1,0:T(8,128)(2,1)}) %all-reduce.2.cloned.1.call-update) | async-done | bytes 589840 | tf_op jit(solution)/shard_map/psum | solution.py:16
  366.1 1.4 fusion.14
  367.5 44.5 %all-gather.2 = bf16[32,36,256]{2,1,0:T(8,128)(2,1)S(1)} all-gather(bf16[1,36,256]{2,1,0:T(8,128)(2,1)S(1)} %fusion.14), channel_id=1, replica_groups=mesh['clip'=16,'seq'=32] {'seq'}, dimensions={0}, use_global_device_ids=true | all-gather | bytes 608256 | tf_op jit(solution)/shard_map/all_gather | solution.py:89
  412.1 0.8 fusion.34
  412.8 0.7 copy-done.2
  413.7 21.1 %all-gather.12.cloned.1.call-done = bf16[32,36,576]{2,1,0:T(8,128)(2,1)} async-done(((bf16[1,36,576]{2,1,0:T(8,128)(2,1)}), bf16[32,36,576]{2,1,0:T(8,128)(2,1)}) %all-gather.12.cloned.1.call-update) | async-done | bytes 1327120 | tf_op jit(solution)/shard_map/all_gather | solution.py:76
  434.8 3.5 reshape.152
  438.3 62.6 %all-gather.14.cloned.1.call-done = bf16[32,18,1152]{2,1,0:T(8,128)(2,1)} async-done(((bf16[1,18,1152]{2,1,0:T(8,128)(2,1)}), bf16[32,18,1152]{2,1,0:T(8,128)(2,1)}) %all-gather.14.cloned.1.call-update) | async-done | bytes 1327120 | tf_op jit(solution)/shard_map/all_gather | solution.py:77
  500.9 2.4 reshape.156
  503.3 63.6 %all-gather.16.cloned.1.call-done = bf16[32,36,576]{2,1,0:T(8,128)(2,1)} async-done(((bf16[1,36,576]{2,1,0:T(8,128)(2,1)}), bf16[32,36,576]{2,1,0:T(8,128)(2,1)}) %all-gather.16.cloned.1.call-update) | async-done | bytes 1327120 | tf_op jit(solution)/shard_map/all_gather | solution.py:78
  567.0 2.5 reshape.158
  569.5 2.2 fusion.2
  574.1 1.5 fusion.3
  (49 shorter events, 9.0 us)
Async XLA Ops:
  6.5 359.6 %copy-start = (bf16[1152,36]{0,1:T(8,128)(2,1)S(1)}, bf16[1152,36]{0,1:T(8,128)(2,1)}, u32[]{:S(2)}) copy-start(bf16[1152,36]{0,1:T(8,128)(2,1)} %param.15) | copy-start | bytes 248836
  6.5 3.6 copy-start.6
  6.5 3.7 copy-start.1
  6.5 80.8 %all-gather.10.cloned.1.call-start = ((), (), s32[]{:S(2)}) async-start(), calls=%async_computation.3 | async-start | bytes 4257792 | tf_op jit(solution)/shard_map/all_gather | solution.py:71
  7.3 358.8 %all-reduce.2.cloned.1.call-start = ((), (), s32[]{:S(2)}) async-start(), calls=%async_computation.2 | async-start | bytes 1179648 | tf_op jit(solution)/shard_map/psum | solution.py:16
  8.9 425.9 %all-gather.12.cloned.1.call-start = ((), (), s32[]{:S(2)}) async-start(), calls=%async_computation.4 | async-start | bytes 1689600 | tf_op jit(solution)/shard_map/all_gather | solution.py:76
  9.6 491.3 %all-gather.14.cloned.1.call-start = ((), (), s32[]{:S(2)}) async-start(), calls=%async_computation.5 | async-start | bytes 1824768 | tf_op jit(solution)/shard_map/all_gather | solution.py:77
  16.9 12.1 %copy-start.7 = (s32[32]{0:T(128)S(1)}, s32[32]{0:T(128)}, u32[]{:S(2)}) copy-start(s32[32]{0:T(128)} %param.19) | copy-start | bytes 388
  17.9 31.8 %all-to-all-start = ((bf16[32,2,4608]{2,1,0:T(2,128)(2,1)}), bf16[32,2,4608]{2,1,0:T(2,128)(2,1)S(1)}, u32[]{:S(2)}, u32[]{:S(2)}) async-start(bf16[32,2,4608]{2,1,0:T(2,128)(2,1)} %reshape.164), calls=%async_computation | async-start | bytes 1179648 | tf_op jit(solution)/shard_map/all_to_all | solution.py:67
  28.4 538.6 %all-gather.16.cloned.1.call-start = ((), (), s32[]{:S(2)}) async-start(), calls=%async_computation.6 | async-start | bytes 1689600 | tf_op jit(solution)/shard_map/all_gather | solution.py:78
  99.3 1.9 copy-start.4
  104.9 464.5 %all-to-all-start.1 = ((bf16[32,8,576]{2,1,0:T(8,128)(2,1)}), bf16[32,8,576]{2,1,0:T(8,128)(2,1)}, u32[]{:S(2)}, u32[]{:S(2)}) async-start(bf16[32,8,576]{2,1,0:T(8,128)(2,1)} %reshape.135), calls=%async_computation.1 | async-start | bytes 655360 | tf_op jit(solution)/shard_map/all_to_all | solution.py:81
  412.8 0.8 copy-start.2
  571.7 1.0 copy-start.3
  572.6 1.0 copy-start.5
Sparse Core Ops, SparseCore 0:
  9.5 77.7 all-gather.9
  90.3 275.7 all-reduce.1
  368.5 66.2 all-gather.11
  437.0 63.8 all-gather.13
  503.1 63.7 all-gather.15
where the time goes:
time: 583 us; the launch traced here: 582 us
  waiting for transfers between devices  461 us (79%)
  blocking collectives  44.5 us (8%)
  local copies, waits for them, and re-layouts  23.2 us (4%)
  starting transfers between devices  17.4 us (3%)
  between operations  14.1 us (2%)
  matrix products  11.8 us (2%)
  other arithmetic  10.3 us (2%)
    psum x1, waiting for transfers between devices, spread_2(): return lax.psum(block, axis)  254 us
    all_gather x1, waiting for transfers between devices, per_device(): lax.all_gather(cross_out, 'seq', axis=1, tiled=True)  63.6 us
    all_gather x1, waiting for transfers between devices, per_device(): lax.all_gather(cross_query, 'seq', axis=1, tiled=True)  62.6 us
    all_gather x1, blocking collectives, per_device(): keyval = lax.all_gather(own_columns, 'seq', axis=1, tiled=True)  44.5 us
    all_gather x1, waiting for transfers between devices, per_device(): lax.all_gather(self_proj, 'seq', axis=1, tiled=True)  37.1 us
    all_gather x1, waiting for transfers between devices, per_device(): lax.all_gather(self_out, 'seq', axis=1, tiled=True)  21.1 us
    all_to_all x1, waiting for transfers between devices, per_device(): lax.all_to_all(normed, 'seq', split_axis=1, concat_axis=0, tiled=True)  20.2 us
    unnamed x24, local copies, waits for them, and re-layouts  17.1 us
  transfers between devices with their start and end apart: 7, of which 6 were waited for; matrix products, arithmetic and copies ran while one was open for 7% of the time, Pallas kernels for 0%

commit v1 on v0

--- a/solution.py
+++ b/solution.py
@@ -9,11 +9,6 @@
 
 
 EPS = 1e-06
-
-
-def spread_2(block, axis, owner):
-    block = jnp.where(lax.axis_index(axis) == owner, block, jnp.zeros_like(block))
-    return lax.psum(block, axis)
 
 
 def layer_norm(values):
@@ -43,6 +38,22 @@
     return attended.astype(jnp.bfloat16).reshape(frames, patches, attn)
 
 
+def gather_rows(blocks, axis):
+    packed = jnp.concatenate(blocks, axis=0)
+    full = lax.all_gather(packed, axis, axis=0, tiled=False)
+    out, start = [], 0
+    for b in blocks:
+        out.append(full[:, start : start + b.shape[0], :])
+        start += b.shape[0]
+    return out
+
+
+def project(x, gathered):
+    count, cols, _ = gathered.shape
+    y = jnp.einsum("tk,sck->tsc", x, gathered, preferred_element_type=jnp.float32)
+    return y.reshape(x.shape[0], count * cols)
+
+
 def per_device(
     frames_in,
     modulation,
@@ -62,38 +73,65 @@
     scale_q = 1.0 / math.sqrt(HEAD_DIM)
     pix_dev = pixels // count
     frames = frame_rows * count
+    text_len = text_bank.shape[1]
+    txt_dev = text_len // count
+
+    (proj_g,) = gather_rows([self_proj.T], "seq")
+    query_g, keyval_g, so_g, co_g = gather_rows(
+        [
+            cross_query.T,
+            cross_keyval.T,
+            self_out.T.reshape(-1, width),
+            cross_out.T.reshape(-1, width),
+        ],
+        "seq",
+    )
+
     tokens = frames_in.astype(jnp.float32)
     normed = (layer_norm(tokens) * (1.0 + modulation[1]) + modulation[0]).astype(jnp.bfloat16)
-    switched = lax.all_to_all(normed, "seq", split_axis=1, concat_axis=0, tiled=True)
+    send = jnp.concatenate(
+        [
+            normed.reshape(count, pix_dev, width),
+            text_bank[0].reshape(count, txt_dev, width),
+        ],
+        axis=1,
+    )
+    recv = lax.all_to_all(send, "seq", 0, 0, tiled=True)
+    switched = recv[:, :pix_dev, :]
+    pick = prompt_pick[0]
+    memory_rows = lax.dynamic_index_in_dim(recv[:, pix_dev:, :], pick, 0, keepdims=False)
+
     flat_pix = switched.reshape(-1, width)
-    qkv = jnp.dot(
-        flat_pix,
-        lax.all_gather(self_proj, "seq", axis=1, tiled=True),
-        preferred_element_type=jnp.float32,
-    ).astype(jnp.bfloat16)
+    qkv = project(flat_pix, proj_g).astype(jnp.bfloat16)
     qkv = qkv.reshape(frames, pix_dev, 3 * attn)
-    out_self, query_weight, out_cross = (
-        lax.all_gather(self_out, "seq", axis=1, tiled=True),
-        lax.all_gather(cross_query, "seq", axis=1, tiled=True),
-        lax.all_gather(cross_out, "seq", axis=1, tiled=True),
+    attended = temporal_attention(qkv, heads, attn, scale_q)
+
+    keyval_rows = project(memory_rows, keyval_g).astype(jnp.bfloat16)
+    key_rows = head_norm(keyval_rows[:, :attn].astype(jnp.float32), heads).astype(jnp.bfloat16)
+    kv_rows = jnp.concatenate([key_rows.reshape(txt_dev, attn), keyval_rows[:, attn:]], axis=1)
+
+    send2 = jnp.concatenate(
+        [
+            attended.reshape(count, -1),
+            jnp.broadcast_to(kv_rows.reshape(1, -1), (count, txt_dev * 2 * attn)),
+        ],
+        axis=1,
     )
-    attended = temporal_attention(qkv, heads, attn, scale_q)
-    returned = lax.all_to_all(attended, "seq", split_axis=0, concat_axis=1, tiled=True)
-    self_term = jnp.dot(returned.reshape(-1, attn), out_self, preferred_element_type=jnp.float32)
+    recv2 = lax.all_to_all(send2, "seq", 0, 0, tiled=True)
+    returned = recv2[:, : pix_dev * attn].reshape(pixels, attn)
+    keyval = recv2[:, pix_dev * attn :].reshape(text_len, 2 * attn)
+
+    out_self = so_g.reshape(width, attn)
+    out_cross = co_g.reshape(width, attn)
+    self_term = jnp.einsum("ta,ca->tc", returned, out_self, preferred_element_type=jnp.float32)
     after_self = (tokens.reshape(-1, width) + modulation[2] * self_term).astype(jnp.bfloat16)
-    pick = prompt_pick[0]
-    memory = spread_2(text_bank[0], "seq", pick)
-    own_columns = jnp.dot(memory, cross_keyval, preferred_element_type=jnp.float32).astype(
-        jnp.bfloat16
-    )
-    keyval = lax.all_gather(own_columns, "seq", axis=1, tiled=True)
-    text_len = keyval.shape[0]
-    text_key = head_norm(keyval[:, :attn].astype(jnp.float32), heads).astype(jnp.bfloat16)
+
+    text_key = keyval[:, :attn].reshape(text_len, heads, HEAD_DIM)
     text_value = keyval[:, attn:].reshape(text_len, heads, HEAD_DIM)
     slots = jnp.arange(text_lengths.shape[0], dtype=jnp.int32)
     length = jnp.sum(jnp.where(slots == pick, text_lengths, 0))
     live = jnp.arange(text_len, dtype=jnp.int32) < length
-    text_query = jnp.dot(after_self, query_weight, preferred_element_type=jnp.float32)
+    text_query = project(after_self, query_g)
     text_query = (head_norm(text_query, heads) * scale_q).astype(jnp.bfloat16)
     cross_scores = jnp.einsum(
         "thd,lhd->thl", text_query, text_key, preferred_element_type=jnp.float32
@@ -105,7 +143,7 @@
         "thl,lhd->thd", cross_probs, text_value, preferred_element_type=jnp.float32
     )
     crossed = (cross_mix / cross_total[..., None]).astype(jnp.bfloat16).reshape(-1, attn)
-    cross_term = jnp.dot(crossed, out_cross, preferred_element_type=jnp.float32)
+    cross_term = jnp.einsum("ta,ca->tc", crossed, out_cross, preferred_element_type=jnp.float32)
     frames_out = (after_self.astype(jnp.float32) + cross_term).astype(jnp.bfloat16)
     return frames_out.reshape(frame_rows, pixels, width)
 

time: 583 us -> 225 us (0.39)
  waiting for transfers between devices: 461 us -> 136 us
  blocking collectives: 44.5 us -> 0 us
  local copies, waits for them, and re-layouts: 23.2 us -> 36 us
    psum x1 -> x0, waiting for transfers between devices: 254 us -> none  [spread_2(): return lax.psum(block, axis)]
    all_gather x4 -> x2, waiting for transfers between devices: 184 us -> 86.5 us  [gather_rows(): full = lax.all_gather(packed, axis, axis=0, tiled=False)]
    all_gather x1 -> x0, blocking collectives: 44.5 us -> none  [per_device(): keyval = lax.all_gather(own_columns, 'seq', axis=1, tiled=True)]
    all_to_all x2, waiting for transfers between devices: 20.2 us -> 48.8 us  [the longest x1 37.1 us: per_device(): recv = lax.all_to_all(send, 'seq', 0, 0, tiled=True)]
    slice x1 -> x9, local copies, waits for them, and re-layouts: 0.75 us -> 10.3 us  [the longest x2 8.78 us: gather_rows(): out.append(full[:, start:start + b.shape[0], :])]
    unnamed x24 -> x18, local copies, waits for them, and re-layouts: 17.1 us -> 8.26 us
    reshape x1 -> x6, local copies, waits for them, and re-layouts: 1.09 us -> 9.25 us  [the longest x1 3.98 us: per_device(): out_self = so_g.reshape(width, attn)]
  transfers between devices with their start and end apart: 7 -> 4, of which waited for: 6 -> 4; matrix products, arithmetic and copies ran while one was open for 7% -> 16% of each run, Pallas kernels for 0% -> 0%
where the time goes in v1:
time: 225 us; the launch traced here: 224 us
  waiting for transfers between devices  136 us (60%)
  local copies, waits for them, and re-layouts  36 us (16%)
  starting transfers between devices  15.6 us (7%)
  between operations  14.4 us (6%)
  matrix products  12.6 us (6%)
  other arithmetic  9.72 us (4%)
    all_gather x2, waiting for transfers between devices, gather_rows(): full = lax.all_gather(packed, axis, axis=0, tiled=False)  86.5 us
    all_to_all x1, waiting for transfers between devices, per_device(): recv = lax.all_to_all(send, 'seq', 0, 0, tiled=True)  37.1 us
    all_to_all x1, waiting for transfers between devices, per_device(): recv2 = lax.all_to_all(send2, 'seq', 0, 0, tiled=True)  11.6 us
    all_to_all x1, starting transfers between devices, per_device(): recv = lax.all_to_all(send, 'seq', 0, 0, tiled=True)  10.5 us
    slice x2, local copies, waits for them, and re-layouts, gather_rows(): out.append(full[:, start:start + b.shape[0], :])  8.78 us
    unnamed x18, local copies, waits for them, and re-layouts  8.26 us
    dot_general x3, matrix products, project(): jnp.einsum('tk,sck->tsc', x, gathered, preferred_element_type=jnp.float32)  6.66 us
    all_to_all x1, starting transfers between devices, per_device(): recv2 = lax.all_to_all(send2, 'seq', 0, 0, tiled=True)  5.07 us
  transfers between devices with their start and end apart: 4, of which 4 were waited for; matrix products, arithmetic and copies ran while one was open for 16% of the time, Pallas kernels for 0%

profile of v1, /device:TPU:1, one launch (start us, length us, event | category | flops | bytes accessed | tf_op | source)
XLA Modules:
  0.0 224.4 jit_solution(6052000259257361172)
XLA Ops:
  6.5 0.7 all-gather.7.cloned.1.call-update
  7.3 0.9 reshape.147
  8.2 0.9 reshape.148
  9.1 1.7 maximum_bitcast_fusion.1
  10.9 0.9 slice_reduce_fusion.1
  12.6 1.1 pad_maximum_fusion
  13.7 10.5 %all-to-all-start = ((bf16[32,16,1152]{2,1,0:T(8,128)(2,1)}), bf16[32,16,1152]{2,1,0:T(8,128)(2,1)S(1)}, u32[]{:S(2)}, u32[]{:S(2)}) async-start(bf16[32,16,1152]{2,1,0:T(8,128)(2,1)} %pad_maximum_fusion), calls=%async_computation | async-start | bytes 2359296 | tf_op jit(solution)/shard_map/all_to_all | solution.py:99
  24.8 37.1 %all-to-all-done = bf16[32,16,1152]{2,1,0:T(8,128)(2,1)S(1)} async-done(((bf16[32,16,1152]{2,1,0:T(8,128)(2,1)}), bf16[32,16,1152]{2,1,0:T(8,128)(2,1)S(1)}, u32[]{:S(2)}, u32[]{:S(2)}) %all-to-all-start) | async-done | bytes 1179680 | tf_op jit(solution)/shard_map/all_to_all | solution.py:99
  61.9 0.9 slice.76
  62.8 28.7 %all-gather.7.cloned.1.call-done = bf16[32,54,1152]{2,1,0:T(8,128)(2,1)} async-done(((bf16[1,54,1152]{2,1,0:T(8,128)(2,1)}), bf16[32,54,1152]{2,1,0:T(8,128)(2,1)}) %all-gather.7.cloned.1.call-update) | async-done | bytes 3981328 | tf_op jit(solution)/shard_map/all_gather | solution.py:43
  91.5 5.0 %reshape.165 = bf16[1728,1152]{1,0:T(8,128)(2,1)} reshape(bf16[32,54,1152]{2,1,0:T(8,128)(2,1)} %all-gather.7.cloned.1.call-done) | data formatting | bytes 7962624
  96.5 3.5 %convolution_convert_fusion = bf16[256,1728]{0,1:T(8,128)(2,1)S(1)} fusion(bf16[1728,1152]{1,0:T(8,128)(2,1)} %reshape.165, bf16[32,16,1152]{2,1,0:T(8,128)(2,1)S(1)} %all-to-all-done), kind=kOutput, calls=%fused_computation.4 | convolution fusion | flops 1019658240 | bytes 5455872 | tf_op jit(solution)/shard_map/tk,sck->tsc/dot_general | solution.py:53
  100.6 0.9 slice_convert_fusion.1
  102.5 1.5 reshape.142
  104.8 0.7 multiply_convert_fusion
  105.5 0.9 fusion.36
  107.3 1.4 reshape_reshape.6
  108.7 57.8 %all-gather.9.cloned.1.call-done = bf16[32,90,1152]{2,1,0:T(8,128)(2,1)} async-done(((bf16[1,90,1152]{2,1,0:T(8,128)(2,1)}), bf16[32,90,1152]{2,1,0:T(8,128)(2,1)}) %all-gather.9.cloned.1.call-update) | async-done | bytes 6635536 | tf_op jit(solution)/shard_map/all_gather | solution.py:43
  166.5 3.5 %slice.77 = bf16[32,36,1152]{2,1,0:T(8,128)(2,1)S(1)} slice(bf16[32,90,1152]{2,1,0:T(8,128)(2,1)} %all-gather.9.cloned.1.call-done), slice={[0:32], [18:54], [0:1152]} | slice | bytes 5308416 | tf_op jit(solution)/shard_map/slice | solution.py:46
  170.0 2.3 %dot_general.35 = bf16[1152,1152]{1,0:T(8,128)(2,1)} reshape(bf16[32,36,1152]{2,1,0:T(8,128)(2,1)S(1)} %slice.77) | data formatting | bytes 5308416 | tf_op jit(solution)/shard_map/tk,sck->tsc/dot_general | solution.py:53
  172.3 2.6 %convolution_convert_fusion.1 = bf16[8,1152]{1,0:T(8,128)(2,1)S(1)} fusion(bf16[1152,1152]{1,0:T(8,128)(2,1)} %dot_general.35, bf16[32,8,1152]{2,1,0:T(8,128)(2,1)} %slice.76, s32[]{:T(128)S(6)} %select_n.15), kind=kOutput, calls=%fused_computation.7 | convolution fusion | flops 21242880 | bytes 2691076 | tf_op jit(solution)/shard_map/tk,sck->tsc/dot_general | solution.py:53
  176.1 1.3 reduce.10
  177.4 1.1 reshape.176
  178.6 5.1 %all-to-all-start.1 = ((bf16[32,2,6912]{2,1,0:T(2,128)(2,1)}), bf16[32,2,6912]{2,1,0:T(2,128)(2,1)S(1)}, u32[]{:S(2)}, u32[]{:S(2)}) async-start(bf16[32,2,6912]{2,1,0:T(2,128)(2,1)} %reshape.176), calls=%async_computation.1 | async-start | bytes 1769472 | tf_op jit(solution)/shard_map/all_to_all | solution.py:120
  185.0 5.3 %fusion.34 = (bf16[32,18,1152]{2,1,0:T(8,128)(2,1)S(1)}, bf16[32,18,1152]{2,1,0:T(8,128)(2,1)}, bf16[32,18,1152]{2,1,0:T(8,128)(2,1)}) fusion(bf16[32,90,1152]{2,1,0:T(8,128)(2,1)} %all-gather.9.cloned.1.call-done), kind=kLoop, calls=%fused_computation.74 | loop fusion | bytes 7962624 | tf_op jit(solution)/shard_map/slice | solution.py:46
  190.3 4.0 %reshape.150 = bf16[1152,576]{1,0:T(8,128)(2,1)} reshape(bf16[32,18,1152]{2,1,0:T(8,128)(2,1)} %get-tuple-element.10) | data formatting | bytes 2654208 | tf_op jit(solution)/shard_map/reshape | solution.py:124
  194.2 2.2 reshape.155
  196.4 11.6 %all-to-all-done.1 = bf16[32,2,6912]{2,1,0:T(2,128)(2,1)S(1)} async-done(((bf16[32,2,6912]{2,1,0:T(2,128)(2,1)}), bf16[32,2,6912]{2,1,0:T(2,128)(2,1)S(1)}, u32[]{:S(2)}, u32[]{:S(2)}) %all-to-all-start.1) | async-done | bytes 884768 | tf_op jit(solution)/shard_map/all_to_all | solution.py:120
  209.0 1.0 reshape.149
  210.4 1.8 fusion.2
  215.1 0.9 copy-done.1
  216.0 1.5 fusion.3
  (61 shorter events, 10.7 us)
Async XLA Ops:
  6.5 5.2 %copy-start = (bf16[1,256,1152]{2,1,0:T(8,128)(2,1)S(1)}, bf16[1,256,1152]{2,1,0:T(8,128)(2,1)}, u32[]{:S(2)}) copy-start(bf16[1,256,1152]{2,1,0:T(8,128)(2,1)} %param.10) | copy-start | bytes 1769476
  6.5 84.9 %all-gather.7.cloned.1.call-start = ((), (), s32[]{:S(2)}) async-start(), calls=%async_computation.2 | async-start | bytes 4257792 | tf_op jit(solution)/shard_map/all_gather | solution.py:43
  7.3 159.3 %all-gather.9.cloned.1.call-start = ((), (), s32[]{:S(2)}) async-start(), calls=%async_computation.3 | async-start | bytes 7299072 | tf_op jit(solution)/shard_map/all_gather | solution.py:43
  9.1 3.4 %copy-start.5 = (bf16[1,256,1152]{2,1,0:T(8,128)(2,1)S(1)}, bf16[1,256,1152]{2,1,0:T(8,128)(2,1)}, u32[]{:S(2)}) copy-start(bf16[1,256,1152]{2,1,0:T(8,128)(2,1)} %param.17) | copy-start | bytes 1769476
  13.7 48.3 %all-to-all-start = ((bf16[32,16,1152]{2,1,0:T(8,128)(2,1)}), bf16[32,16,1152]{2,1,0:T(8,128)(2,1)S(1)}, u32[]{:S(2)}, u32[]{:S(2)}) async-start(bf16[32,16,1152]{2,1,0:T(8,128)(2,1)} %pad_maximum_fusion), calls=%async_computation | async-start | bytes 2359296 | tf_op jit(solution)/shard_map/all_to_all | solution.py:99
  172.3 3.2 %copy-start.4 = (bf16[32,4608]{1,0:T(8,128)(2,1)S(1)}, bf16[32,4608]{1,0:T(8,128)(2,1)}, u32[]{:S(2)}) copy-start(bf16[32,4608]{1,0:T(8,128)(2,1)} %reshape_reshape.6) | copy-start | bytes 884740
  177.4 6.2 %copy-start.6 = (s32[32]{0:T(128)S(1)}, s32[32]{0:T(128)}, u32[]{:S(2)}) copy-start(s32[32]{0:T(128)} %param.19) | copy-start | bytes 388
  178.6 29.5 %all-to-all-start.1 = ((bf16[32,2,6912]{2,1,0:T(2,128)(2,1)}), bf16[32,2,6912]{2,1,0:T(2,128)(2,1)S(1)}, u32[]{:S(2)}, u32[]{:S(2)}) async-start(bf16[32,2,6912]{2,1,0:T(2,128)(2,1)} %reshape.176), calls=%async_computation.1 | async-start | bytes 1769472 | tf_op jit(solution)/shard_map/all_to_all | solution.py:120
  208.9 1.5 copy-start.2
  210.4 1.8 copy-start.3
  214.6 1.4 copy-start.1
Sparse Core Ops, SparseCore 0:
  9.5 81.9 all-gather.6
  93.6 72.8 all-gather.8

commit v2 on v1

--- a/solution.py
+++ b/solution.py
@@ -38,20 +38,29 @@
     return attended.astype(jnp.bfloat16).reshape(frames, patches, attn)
 
 
-def gather_rows(blocks, axis):
-    packed = jnp.concatenate(blocks, axis=0)
-    full = lax.all_gather(packed, axis, axis=0, tiled=False)
-    out, start = [], 0
-    for b in blocks:
-        out.append(full[:, start : start + b.shape[0], :])
-        start += b.shape[0]
-    return out
+def pack_rows(pieces):
+    total = sum(p.shape[1] for p in pieces)
+    eye = jnp.eye(total, dtype=pieces[0].dtype)
+    packed, start = None, 0
+    for p in pieces:
+        part = jnp.einsum(
+            "rc,kc->rk", eye[:, start : start + p.shape[1]], p, preferred_element_type=jnp.float32
+        )
+        packed = part if packed is None else packed + part
+        start += p.shape[1]
+    return packed.astype(pieces[0].dtype)
 
 
 def project(x, gathered):
     count, cols, _ = gathered.shape
     y = jnp.einsum("tk,sck->tsc", x, gathered, preferred_element_type=jnp.float32)
     return y.reshape(x.shape[0], count * cols)
+
+
+def project_block(x, gathered, start, cols):
+    count, rows, _ = gathered.shape
+    y = jnp.einsum("tk,sck->tsc", x, gathered, preferred_element_type=jnp.float32)
+    return y[:, :, start : start + cols].reshape(x.shape[0], count * cols)
 
 
 def per_device(
@@ -76,16 +85,15 @@
     text_len = text_bank.shape[1]
     txt_dev = text_len // count
 
-    (proj_g,) = gather_rows([self_proj.T], "seq")
-    query_g, keyval_g, so_g, co_g = gather_rows(
-        [
-            cross_query.T,
-            cross_keyval.T,
-            self_out.T.reshape(-1, width),
-            cross_out.T.reshape(-1, width),
-        ],
-        "seq",
-    )
+    outs_pair = jnp.concatenate([self_out, cross_out], axis=0)
+    sizes = (self_proj.shape[1], cross_keyval.shape[1], cross_query.shape[1], outs_pair.shape[1])
+    packed = pack_rows([self_proj, cross_keyval, cross_query, outs_pair])
+    gathered = lax.all_gather(packed, "seq", axis=0, tiled=False)
+    kv_at = sizes[0]
+    q_at = kv_at + sizes[1]
+    outs_at = q_at + sizes[2]
+    query_g = gathered[:, q_at : q_at + sizes[2], :]
+    outs_g = gathered[:, outs_at : outs_at + sizes[3], :]
 
     tokens = frames_in.astype(jnp.float32)
     normed = (layer_norm(tokens) * (1.0 + modulation[1]) + modulation[0]).astype(jnp.bfloat16)
@@ -102,11 +110,11 @@
     memory_rows = lax.dynamic_index_in_dim(recv[:, pix_dev:, :], pick, 0, keepdims=False)
 
     flat_pix = switched.reshape(-1, width)
-    qkv = project(flat_pix, proj_g).astype(jnp.bfloat16)
+    qkv = project_block(flat_pix, gathered, 0, sizes[0]).astype(jnp.bfloat16)
     qkv = qkv.reshape(frames, pix_dev, 3 * attn)
     attended = temporal_attention(qkv, heads, attn, scale_q)
 
-    keyval_rows = project(memory_rows, keyval_g).astype(jnp.bfloat16)
+    keyval_rows = project_block(memory_rows, gathered, kv_at, sizes[1]).astype(jnp.bfloat16)
     key_rows = head_norm(keyval_rows[:, :attn].astype(jnp.float32), heads).astype(jnp.bfloat16)
     kv_rows = jnp.concatenate([key_rows.reshape(txt_dev, attn), keyval_rows[:, attn:]], axis=1)
 
@@ -121,8 +129,8 @@
     returned = recv2[:, : pix_dev * attn].reshape(pixels, attn)
     keyval = recv2[:, pix_dev * attn :].reshape(text_len, 2 * attn)
 
-    out_self = so_g.reshape(width, attn)
-    out_cross = co_g.reshape(width, attn)
+    out_self = outs_g[:, :, :attn].reshape(-1, attn)
+    out_cross = outs_g[:, :, attn:].reshape(-1, attn)
     self_term = jnp.einsum("ta,ca->tc", returned, out_self, preferred_element_type=jnp.float32)
     after_self = (tokens.reshape(-1, width) + modulation[2] * self_term).astype(jnp.bfloat16)
 

time: 225 us -> 195 us (0.87)
  waiting for transfers between devices: 136 us -> 94.2 us
  matrix products: 12.6 us -> 22.6 us
  local copies, waits for them, and re-layouts: 36 us -> 38.3 us
    all_gather x2 -> x1, waiting for transfers between devices: 86.5 us -> 46.6 us  [per_device(): gathered = lax.all_gather(packed, 'seq', axis=0, tiled=False)]
    dot_general x0 -> x6, matrix products: none -> 17.2 us  [the longest x2 14.4 us: project_block(): jnp.einsum('tk,sck->tsc', x, gathered, preferred_element_type=jnp.float32)]
    dot_general x3 -> x1, matrix products: 6.66 us -> 0.59 us  [project(): jnp.einsum('tk,sck->tsc', x, gathered, preferred_element_type=jnp.float32)]
    slice x2 -> x6, local copies, waits for them, and re-layouts: 8.78 us -> 13.6 us  [the longest x4 5.41 us: project_block(): return y[:, :, start:start + cols].reshape(x.shape[0], count * cols)]
    convert_element_type x1 -> x2, local copies, waits for them, and re-layouts: 0.61 us -> 4.71 us  [the longest x1 4.57 us: per_device(): qkv = project_block(flat_pix, gathered, 0, sizes[0]).astype(jnp.bfloat16)]
    reshape x4 -> x2, local copies, waits for them, and re-layouts: 7.99 us -> 5.07 us  [the longest x1 3.55 us: per_device(): out_cross = outs_g[:, :, attn:].reshape(-1, attn)]
    slice x2, local copies, waits for them, and re-layouts: 0.31 us -> 2.69 us  [per_device(): text_key = keyval[:, :attn].reshape(text_len, heads, HEAD_DIM)]
    dot_general x2 -> x1, local copies, waits for them, and re-layouts: 2.63 us -> 0.35 us  [project(): jnp.einsum('tk,sck->tsc', x, gathered, preferred_element_type=jnp.float32)]
  transfers between devices with their start and end apart: 4 -> 3, of which waited for: 4 -> 3; matrix products, arithmetic and copies ran while one was open for 16% -> 9% of each run, Pallas kernels for 0% -> 0%
where the time goes in v2:
time: 195 us; the launch traced here: 194 us
  waiting for transfers between devices  94.2 us (48%)
  local copies, waits for them, and re-layouts  38.3 us (20%)
  matrix products  22.6 us (12%)
  starting transfers between devices  15.8 us (8%)
  between operations  14.5 us (7%)
  other arithmetic  8.52 us (4%)
    all_gather x1, waiting for transfers between devices, per_device(): gathered = lax.all_gather(packed, 'seq', axis=0, tiled=False)  46.6 us
    all_to_all x1, waiting for transfers between devices, per_device(): recv = lax.all_to_all(send, 'seq', 0, 0, tiled=True)  37.8 us
    dot_general x2, matrix products, project_block(): jnp.einsum('tk,sck->tsc', x, gathered, preferred_element_type=jnp.float32)  14.4 us
    all_to_all x1, starting transfers between devices, per_device(): recv = lax.all_to_all(send, 'seq', 0, 0, tiled=True)  10.5 us
    all_to_all x1, waiting for transfers between devices, per_device(): recv2 = lax.all_to_all(send2, 'seq', 0, 0, tiled=True)  9.81 us
    unnamed x33, local copies, waits for them, and re-layouts  6.15 us
    slice x4, local copies, waits for them, and re-layouts, project_block(): return y[:, :, start:start + cols].reshape(x.shape[0], count * cols)  5.41 us
    all_to_all x1, starting transfers between devices, per_device(): recv2 = lax.all_to_all(send2, 'seq', 0, 0, tiled=True)  5.36 us
  transfers between devices with their start and end apart: 3, of which 3 were waited for; matrix products, arithmetic and copies ran while one was open for 9% of the time, Pallas kernels for 0%

profile of v2, /device:TPU:1, one launch (start us, length us, event | category | flops | bytes accessed | tf_op | source)
XLA Modules:
  0.0 194.0 jit_solution(12603078085272443876)
XLA Ops:
  6.6 0.9 copy-done
  7.7 1.2 convolution_add_fusion.3
  9.3 1.0 fusion.4
  11.3 1.1 pad_maximum_fusion
  12.5 10.5 %all-to-all-start = ((bf16[32,16,1152]{2,1,0:T(8,128)(2,1)}), bf16[32,16,1152]{2,1,0:T(8,128)(2,1)S(1)}, u32[]{:S(2)}, u32[]{:S(2)}) async-start(bf16[32,16,1152]{2,1,0:T(8,128)(2,1)} %pad_maximum_fusion), calls=%async_computation | async-start | bytes 2359296 | tf_op jit(solution)/shard_map/all_to_all | solution.py:107
  23.6 37.8 %all-to-all-done = bf16[32,16,1152]{2,1,0:T(8,128)(2,1)S(1)} async-done(((bf16[32,16,1152]{2,1,0:T(8,128)(2,1)}), bf16[32,16,1152]{2,1,0:T(8,128)(2,1)S(1)}, u32[]{:S(2)}, u32[]{:S(2)}) %all-to-all-start) | async-done | bytes 1179680 | tf_op jit(solution)/shard_map/all_to_all | solution.py:107
  61.5 46.6 %all-gather.3.cloned.1.call-done = bf16[4608,1152]{1,0:T(8,128)(2,1)} async-done(((bf16[144,1152]{1,0:T(8,128)(2,1)}), bf16[4608,1152]{1,0:T(8,128)(2,1)}) %all-gather.3.cloned.1.call-update) | async-done | bytes 10616848 | tf_op jit(solution)/shard_map/all_gather | solution.py:91
  108.1 7.1 %fusion.38 = bf16[8,32,144]{2,0,1:T(8,128)(2,1)S(1)} fusion(bf16[32,144,1152]{2,1,0:T(8,128)(2,1)} %bitcast.72, bf16[32,8,1152]{2,1,0:T(8,128)(2,1)S(1)} %slice.106, s32[]{:T(128)S(6)} %select_n.15), kind=kOutput, calls=%fused_computation.72 | convolution fusion | flops 84934656 | bytes 10708996 | tf_op jit(solution)/shard_map/tk,sck->tsc/dot_general | solution.py:62
  116.1 7.3 %fusion.20 = bf16[256,32,144]{0,2,1:T(8,128)(2,1)S(1)} fusion(bf16[32,144,1152]{2,1,0:T(8,128)(2,1)} %bitcast.73, bf16[32,16,1152]{2,1,0:T(8,128)(2,1)S(1)} %all-to-all-done), kind=kOutput, calls=%fused_computation.43 | convolution fusion | flops 2717908992 | bytes 13565952 | tf_op jit(solution)/shard_map/tk,sck->tsc/dot_general | solution.py:62
  123.3 1.0 slice.136
  124.3 4.3 %copy.38 = bf16[256,32,54]{2,1,0:T(8,128)(2,1)S(1)} copy(bf16[256,32,54]{0,2,1:T(8,128)(2,1)} %slice.136) | data formatting | bytes 1769472 | tf_op jit(solution)/shard_map/slice | solution.py:63
  128.6 4.6 %convert_element_type.61 = bf16[32,8,1728]{2,1,0:T(8,128)(2,1)} reshape(bf16[256,32,54]{2,1,0:T(8,128)(2,1)S(1)} %copy.38) | data formatting | bytes 1769472 | tf_op jit(solution)/shard_map/convert_element_type | solution.py:113
  133.2 1.4 slice_convert_fusion.2
  136.1 1.3 reshape.134
  138.9 0.9 multiply_convert_fusion
  139.8 0.9 fusion.48
  140.8 0.7 fusion.10
  143.0 1.3 reduce.10
  144.3 1.1 reshape.161
  145.4 5.4 %all-to-all-start.1 = ((bf16[32,2,6912]{2,1,0:T(2,128)(2,1)}), bf16[32,2,6912]{2,1,0:T(2,128)(2,1)S(1)}, u32[]{:S(2)}, u32[]{:S(2)}) async-start(bf16[32,2,6912]{2,1,0:T(2,128)(2,1)} %reshape.161), calls=%async_computation.1 | async-start | bytes 1769472 | tf_op jit(solution)/shard_map/all_to_all | solution.py:128
  152.1 3.6 %slice.115 = bf16[32,18,1152]{2,1,0:T(8,128)(2,1)} slice(bf16[32,144,1152]{2,1,0:T(8,128)(2,1)} %bitcast.74), slice={[0:32], [90:108], [0:1152]} | slice | bytes 2654208 | tf_op jit(solution)/shard_map/slice | solution.py:95
  155.7 4.6 %fusion.46 = (bf16[32,36,576]{2,1,0:T(8,128)(2,1)}, bf16[32,36,576]{2,1,0:T(8,128)(2,1)S(1)}) fusion(bf16[32,144,1152]{2,1,0:T(8,128)(2,1)} %bitcast.75), kind=kLoop, calls=%fused_computation.89 | loop fusion | bytes 5308416 | tf_op jit(solution)/shard_map/slice | solution.py:133
  160.3 3.5 %reshape.145 = bf16[1152,576]{1,0:T(8,128)(2,1)} reshape(bf16[32,36,576]{2,1,0:T(8,128)(2,1)} %get-tuple-element.8) | data formatting | bytes 2654208 | tf_op jit(solution)/shard_map/reshape | solution.py:133
  163.9 1.5 reshape.140
  165.4 9.8 %all-to-all-done.1 = bf16[32,2,6912]{2,1,0:T(2,128)(2,1)S(1)} async-done(((bf16[32,2,6912]{2,1,0:T(2,128)(2,1)}), bf16[32,2,6912]{2,1,0:T(2,128)(2,1)S(1)}, u32[]{:S(2)}, u32[]{:S(2)}) %all-to-all-start.1) | async-done | bytes 884768 | tf_op jit(solution)/shard_map/all_to_all | solution.py:128
  175.2 0.7 reshape.162
  176.7 0.8 fusion.47
  177.5 1.9 copy.47
  179.3 0.9 copy.46
  180.9 0.8 copy-done.4
  184.7 0.9 copy-done.2
  185.6 1.5 fusion.3
  (79 shorter events, 12.5 us)
Async XLA Ops:
  6.5 0.9 copy-start
  6.5 2.4 %copy-start.10 = (bf16[1152,18]{0,1:T(8,128)(2,1)S(1)}, bf16[1152,18]{0,1:T(8,128)(2,1)}, u32[]{:S(2)}) copy-start(bf16[1152,18]{0,1:T(8,128)(2,1)} %param.14) | copy-start | bytes 124420
  6.5 101.5 %all-gather.3.cloned.1.call-start = ((), (), s32[]{:S(2)}) async-start(), calls=%async_computation.2 | async-start | bytes 10948608 | tf_op jit(solution)/shard_map/all_gather | solution.py:91
  7.7 1.6 copy-start.11
  7.7 1.6 copy-start.12
  8.9 1.4 copy-start.13
  8.9 1.4 copy-start.1
  10.3 1.1 copy-start.6
  12.5 48.9 %all-to-all-start = ((bf16[32,16,1152]{2,1,0:T(8,128)(2,1)}), bf16[32,16,1152]{2,1,0:T(8,128)(2,1)S(1)}, u32[]{:S(2)}, u32[]{:S(2)}) async-start(bf16[32,16,1152]{2,1,0:T(8,128)(2,1)} %pad_maximum_fusion), calls=%async_computation | async-start | bytes 2359296 | tf_op jit(solution)/shard_map/all_to_all | solution.py:107
  137.9 0.9 copy-start.8
  139.7 1.0 copy-start.7
  144.3 6.5 %copy-start.14 = (s32[32]{0:T(128)S(1)}, s32[32]{0:T(128)}, u32[]{:S(2)}) copy-start(s32[32]{0:T(128)} %param.19) | copy-start | bytes 388
  145.4 29.8 %all-to-all-start.1 = ((bf16[32,2,6912]{2,1,0:T(2,128)(2,1)}), bf16[32,2,6912]{2,1,0:T(2,128)(2,1)S(1)}, u32[]{:S(2)}, u32[]{:S(2)}) async-start(bf16[32,2,6912]{2,1,0:T(2,128)(2,1)} %reshape.161), calls=%async_computation.1 | async-start | bytes 1769472 | tf_op jit(solution)/shard_map/all_to_all | solution.py:128
  176.4 3.9 %copy-start.3 = (bf16[1152,576]{1,0:T(8,128)(2,1)S(1)}, bf16[1152,576]{1,0:T(8,128)(2,1)}, u32[]{:S(2)}) copy-start(bf16[1152,576]{1,0:T(8,128)(2,1)} %reshape.140) | copy-start | bytes 3981316
  180.2 1.5 copy-start.4
  182.3 1.0 copy-start.5
  183.3 1.0 copy-start.9
  184.2 1.4 copy-start.2
Sparse Core Ops, SparseCore 0:
  10.4 97.5 all-gather.2

commit v3 on v2

--- a/solution.py
+++ b/solution.py
@@ -57,12 +57,6 @@
     return y.reshape(x.shape[0], count * cols)
 
 
-def project_block(x, gathered, start, cols):
-    count, rows, _ = gathered.shape
-    y = jnp.einsum("tk,sck->tsc", x, gathered, preferred_element_type=jnp.float32)
-    return y[:, :, start : start + cols].reshape(x.shape[0], count * cols)
-
-
 def per_device(
     frames_in,
     modulation,
@@ -110,11 +104,14 @@
     memory_rows = lax.dynamic_index_in_dim(recv[:, pix_dev:, :], pick, 0, keepdims=False)
 
     flat_pix = switched.reshape(-1, width)
-    qkv = project_block(flat_pix, gathered, 0, sizes[0]).astype(jnp.bfloat16)
+    both = jnp.concatenate([flat_pix, memory_rows], axis=0)
+    both_out = jnp.einsum("tk,sck->tsc", both, gathered, preferred_element_type=jnp.float32)
+    tok = flat_pix.shape[0]
+    qkv = both_out[:tok, :, : sizes[0]].reshape(tok, -1).astype(jnp.bfloat16)
     qkv = qkv.reshape(frames, pix_dev, 3 * attn)
     attended = temporal_attention(qkv, heads, attn, scale_q)
 
-    keyval_rows = project_block(memory_rows, gathered, kv_at, sizes[1]).astype(jnp.bfloat16)
+    keyval_rows = both_out[tok:, :, kv_at : kv_at + sizes[1]].reshape(txt_dev, -1).astype(jnp.bfloat16)
     key_rows = head_norm(keyval_rows[:, :attn].astype(jnp.float32), heads).astype(jnp.bfloat16)
     kv_rows = jnp.concatenate([key_rows.reshape(txt_dev, attn), keyval_rows[:, attn:]], axis=1)
 

time: 195 us -> 189 us (0.969)
  matrix products: 22.6 us -> 18.4 us
  local copies, waits for them, and re-layouts: 38.3 us -> 35.2 us
  other arithmetic: 8.52 us -> 10.7 us
    dot_general x2 -> x1, matrix products: 14.4 us -> 9.11 us  [per_device(): jnp.einsum('tk,sck->tsc', both, gathered, preferred_element_type=jnp.floa...]
    slice x2, local copies, waits for them, and re-layouts: 2.69 us -> 0.31 us  [per_device(): text_key = keyval[:, :attn].reshape(text_len, heads, HEAD_DIM)]
    reshape x1, local copies, waits for them, and re-layouts: 3.55 us -> 1.52 us  [per_device(): out_cross = outs_g[:, :, attn:].reshape(-1, attn)]
    reshape x1, local copies, waits for them, and re-layouts: 1.52 us -> 3.55 us  [per_device(): out_self = outs_g[:, :, :attn].reshape(-1, attn)]
    unnamed x33 -> x31, local copies, waits for them, and re-layouts: 6.15 us -> 4.42 us
    slice x5 -> x4, local copies, waits for them, and re-layouts: 5.46 us -> 5.68 us  [the longest x2 5.29 us: per_device(): qkv = both_out[:tok, :, :sizes[0]].reshape(tok, -1).astype(jnp.bfloat16)]
where the time goes in v3:
time: 189 us; the launch traced here: 188 us
  waiting for transfers between devices  93.5 us (49%)
  local copies, waits for them, and re-layouts  35.2 us (19%)
  matrix products  18.4 us (10%)
  starting transfers between devices  15.8 us (8%)
  between operations  14.5 us (8%)
  other arithmetic  10.7 us (6%)
    all_gather x1, waiting for transfers between devices, per_device(): gathered = lax.all_gather(packed, 'seq', axis=0, tiled=False)  46.5 us
    all_to_all x1, waiting for transfers between devices, per_device(): recv = lax.all_to_all(send, 'seq', 0, 0, tiled=True)  37.8 us
    all_to_all x1, starting transfers between devices, per_device(): recv = lax.all_to_all(send, 'seq', 0, 0, tiled=True)  10.5 us
    all_to_all x1, waiting for transfers between devices, per_device(): recv2 = lax.all_to_all(send2, 'seq', 0, 0, tiled=True)  9.15 us
    dot_general x1, matrix products, per_device(): jnp.einsum('tk,sck->tsc', both, gathered, preferred_element_type=jnp.floa...  9.11 us
    all_to_all x1, starting transfers between devices, per_device(): recv2 = lax.all_to_all(send2, 'seq', 0, 0, tiled=True)  5.36 us
    slice x2, local copies, waits for them, and re-layouts, per_device(): qkv = both_out[:tok, :, :sizes[0]].reshape(tok, -1).astype(jnp.bfloat16)  5.29 us
    slice x1, local copies, waits for them, and re-layouts, per_device(): out_cross = outs_g[:, :, attn:].reshape(-1, attn)  5.28 us
  transfers between devices with their start and end apart: 3, of which 3 were waited for; matrix products, arithmetic and copies ran while one was open for 9% of the time, Pallas kernels for 0%

profile of v3, /device:TPU:1, one launch (start us, length us, event | category | flops | bytes accessed | tf_op | source)
XLA Modules:
  0.0 188.2 jit_solution(598815505120280276)
XLA Ops:
  6.6 0.9 copy-done
  7.7 1.2 convolution_add_fusion.3
  9.3 1.0 fusion.4
  11.3 1.1 pad_maximum_fusion
  12.5 10.5 %all-to-all-start = ((bf16[32,16,1152]{2,1,0:T(8,128)(2,1)}), bf16[32,16,1152]{2,1,0:T(8,128)(2,1)S(1)}, u32[]{:S(2)}, u32[]{:S(2)}) async-start(bf16[32,16,1152]{2,1,0:T(8,128)(2,1)} %pad_maximum_fusion), calls=%async_computation | async-start | bytes 2359296 | tf_op jit(solution)/shard_map/all_to_all | solution.py:101
  23.6 37.8 %all-to-all-done = bf16[32,16,1152]{2,1,0:T(8,128)(2,1)S(1)} async-done(((bf16[32,16,1152]{2,1,0:T(8,128)(2,1)}), bf16[32,16,1152]{2,1,0:T(8,128)(2,1)S(1)}, u32[]{:S(2)}, u32[]{:S(2)}) %all-to-all-start) | async-done | bytes 1179680 | tf_op jit(solution)/shard_map/all_to_all | solution.py:101
  61.5 46.5 %all-gather.3.cloned.1.call-done = bf16[4608,1152]{1,0:T(8,128)(2,1)} async-done(((bf16[144,1152]{1,0:T(8,128)(2,1)}), bf16[4608,1152]{1,0:T(8,128)(2,1)}) %all-gather.3.cloned.1.call-update) | async-done | bytes 10616848 | tf_op jit(solution)/shard_map/all_gather | solution.py:85
  108.1 9.1 %convolution_convert_fusion = bf16[264,32,144]{0,2,1:T(8,128)(2,1)S(1)} fusion(bf16[32,144,1152]{2,1,0:T(8,128)(2,1)} %bitcast.71, bf16[8,1152]{1,0:T(8,128)(2,1)S(1)} %dynamic-slice_bitcast_fusion, bf16[256,1152]{1,0:T(8,128)(2,1)S(1)} %get-tuple-element.10), kind=kOutput, calls=%fused_computation.9 | convolution fusion | flops 2805276672 | bytes 13658112 | tf_op jit(solution)/shard_map/tk,sck->tsc/dot_general | solution.py:108
  117.2 1.0 slice.103
  118.8 4.3 %copy.38 = bf16[256,32,54]{2,1,0:T(8,128)(2,1)S(1)} copy(bf16[256,32,54]{0,2,1:T(8,128)(2,1)} %slice.103) | data formatting | bytes 1769472 | tf_op jit(solution)/shard_map/slice | solution.py:110
  123.1 4.6 %convert_element_type.61 = bf16[32,8,1728]{2,1,0:T(8,128)(2,1)} reshape(bf16[256,32,54]{2,1,0:T(8,128)(2,1)S(1)} %copy.38) | data formatting | bytes 1769472 | tf_op jit(solution)/shard_map/convert_element_type | solution.py:110
  127.7 2.1 %slice_convert_fusion.1 = (f32[32,8,576]{2,1,0:T(8,128)S(1)}, f32[32,8,576]{2,1,0:T(8,128)S(1)}, bf16[32,8,576]{2,1,0:T(8,128)(2,1)}) fusion(bf16[32,8,1728]{2,1,0:T(8,128)(2,1)} %convert_element_type.61), kind=kLoop, calls=%fused_computation.54 | loop fusion | flops 294912 | bytes 2359296 | tf_op jit(solution)/shard_map/reshape | solution.py:22
  130.6 0.7 add_rsqrt_fusion
  132.1 0.7 add_rsqrt_fusion.1
  132.8 1.4 reshape.134
  134.2 1.7 multiply_convert_fusion
  135.9 0.9 fusion.46
  136.9 0.7 fusion.10
  137.9 0.7 reshape_reshape.6
  139.6 1.3 reduce.10
  141.0 1.1 reshape.160
  142.1 5.4 %all-to-all-start.1 = ((bf16[32,2,6912]{2,1,0:T(2,128)(2,1)}), bf16[32,2,6912]{2,1,0:T(2,128)(2,1)S(1)}, u32[]{:S(2)}, u32[]{:S(2)}) async-start(bf16[32,2,6912]{2,1,0:T(2,128)(2,1)} %reshape.160), calls=%async_computation.1 | async-start | bytes 1769472 | tf_op jit(solution)/shard_map/all_to_all | solution.py:125
  148.7 3.6 %slice.115 = bf16[32,18,1152]{2,1,0:T(8,128)(2,1)} slice(bf16[32,144,1152]{2,1,0:T(8,128)(2,1)} %bitcast.72), slice={[0:32], [90:108], [0:1152]} | slice | bytes 2654208 | tf_op jit(solution)/shard_map/slice | solution.py:89
  152.4 5.3 %fusion.44 = (bf16[32,36,576]{2,1,0:T(8,128)(2,1)S(1)}, bf16[32,36,576]{2,1,0:T(8,128)(2,1)}) fusion(bf16[32,144,1152]{2,1,0:T(8,128)(2,1)} %bitcast.73), kind=kLoop, calls=%fused_computation.88 | loop fusion | bytes 5308416 | tf_op jit(solution)/shard_map/slice | solution.py:130
  157.6 3.5 %reshape.140 = bf16[1152,576]{1,0:T(8,128)(2,1)} reshape(bf16[32,36,576]{2,1,0:T(8,128)(2,1)} %get-tuple-element.9) | data formatting | bytes 2654208 | tf_op jit(solution)/shard_map/reshape | solution.py:129
  161.2 1.5 reshape.145
  162.7 9.1 %all-to-all-done.1 = bf16[32,2,6912]{2,1,0:T(2,128)(2,1)S(1)} async-done(((bf16[32,2,6912]{2,1,0:T(2,128)(2,1)}), bf16[32,2,6912]{2,1,0:T(2,128)(2,1)S(1)}, u32[]{:S(2)}, u32[]{:S(2)}) %all-to-all-start.1) | async-done | bytes 884768 | tf_op jit(solution)/shard_map/all_to_all | solution.py:125
  171.9 0.7 reshape.161
  172.8 1.0 reshape.139
  174.2 1.8 fusion.2
  178.9 0.9 copy-done.2
  179.8 1.5 fusion.3
  (77 shorter events, 10.1 us)
Async XLA Ops:
  6.5 0.9 copy-start
  6.5 2.4 %copy-start.9 = (bf16[1152,18]{0,1:T(8,128)(2,1)S(1)}, bf16[1152,18]{0,1:T(8,128)(2,1)}, u32[]{:S(2)}) copy-start(bf16[1152,18]{0,1:T(8,128)(2,1)} %param.14) | copy-start | bytes 124420
  6.5 101.5 %all-gather.3.cloned.1.call-start = ((), (), s32[]{:S(2)}) async-start(), calls=%async_computation.2 | async-start | bytes 10948608 | tf_op jit(solution)/shard_map/all_gather | solution.py:85
  7.7 1.6 copy-start.10
  7.7 1.6 copy-start.11
  8.9 1.4 copy-start.12
  8.9 1.4 copy-start.1
  10.3 1.1 copy-start.6
  12.5 48.9 %all-to-all-start = ((bf16[32,16,1152]{2,1,0:T(8,128)(2,1)}), bf16[32,16,1152]{2,1,0:T(8,128)(2,1)S(1)}, u32[]{:S(2)}, u32[]{:S(2)}) async-start(bf16[32,16,1152]{2,1,0:T(8,128)(2,1)} %pad_maximum_fusion), calls=%async_computation | async-start | bytes 2359296 | tf_op jit(solution)/shard_map/all_to_all | solution.py:101
  131.8 1.1 copy-start.5
  131.8 2.4 %copy-start.8 = (f32[32,8,8]{2,1,0:T(8,128)S(1)}, f32[32,8,8]{2,1,0:T(8,128)}, u32[]{:S(2)}) copy-start(f32[32,8,8]{2,1,0:T(8,128)} %add_rsqrt_fusion) | copy-start | bytes 24580
  135.9 1.0 copy-start.7
  141.0 6.5 %copy-start.13 = (s32[32]{0:T(128)S(1)}, s32[32]{0:T(128)}, u32[]{:S(2)}) copy-start(s32[32]{0:T(128)} %param.19) | copy-start | bytes 388
  142.1 29.8 %all-to-all-start.1 = ((bf16[32,2,6912]{2,1,0:T(2,128)(2,1)}), bf16[32,2,6912]{2,1,0:T(2,128)(2,1)S(1)}, u32[]{:S(2)}, u32[]{:S(2)}) async-start(bf16[32,2,6912]{2,1,0:T(2,128)(2,1)} %reshape.160), calls=%async_computation.1 | async-start | bytes 1769472 | tf_op jit(solution)/shard_map/all_to_all | solution.py:125
  172.7 1.5 copy-start.3
  174.2 1.8 copy-start.4
  178.4 1.4 copy-start.2
Sparse Core Ops, SparseCore 0:
  10.4 97.5 all-gather.2

commit v4 on v3

--- a/solution.py
+++ b/solution.py
@@ -80,14 +80,14 @@
     txt_dev = text_len // count
 
     outs_pair = jnp.concatenate([self_out, cross_out], axis=0)
-    sizes = (self_proj.shape[1], cross_keyval.shape[1], cross_query.shape[1], outs_pair.shape[1])
-    packed = pack_rows([self_proj, cross_keyval, cross_query, outs_pair])
+    sizes = (self_proj.shape[1], cross_keyval.shape[1], cross_query.shape[1])
+    pad = -sum(sizes) % 16
+    packed = pack_rows([self_proj, cross_keyval, cross_query, jnp.zeros((width, pad), self_proj.dtype)])
     gathered = lax.all_gather(packed, "seq", axis=0, tiled=False)
     kv_at = sizes[0]
     q_at = kv_at + sizes[1]
-    outs_at = q_at + sizes[2]
     query_g = gathered[:, q_at : q_at + sizes[2], :]
-    outs_g = gathered[:, outs_at : outs_at + sizes[3], :]
+    outs_t = pack_rows([outs_pair])
 
     tokens = frames_in.astype(jnp.float32)
     normed = (layer_norm(tokens) * (1.0 + modulation[1]) + modulation[0]).astype(jnp.bfloat16)
@@ -95,13 +95,15 @@
         [
             normed.reshape(count, pix_dev, width),
             text_bank[0].reshape(count, txt_dev, width),
+            jnp.broadcast_to(outs_t[None], (count,) + outs_t.shape),
         ],
         axis=1,
     )
     recv = lax.all_to_all(send, "seq", 0, 0, tiled=True)
     switched = recv[:, :pix_dev, :]
     pick = prompt_pick[0]
-    memory_rows = lax.dynamic_index_in_dim(recv[:, pix_dev:, :], pick, 0, keepdims=False)
+    memory_rows = lax.dynamic_index_in_dim(recv[:, pix_dev : pix_dev + txt_dev, :], pick, 0, keepdims=False)
+    outs_g = recv[:, pix_dev + txt_dev :, :]
 
     flat_pix = switched.reshape(-1, width)
     both = jnp.concatenate([flat_pix, memory_rows], axis=0)

time: 189 us -> 234 us (1.24)
  waiting for transfers between devices: 93.5 us -> 143 us
  matrix products: 18.4 us -> 13.7 us
    all_to_all x1, waiting for transfers between devices: 37.8 us -> 133 us  [per_device(): recv = lax.all_to_all(send, 'seq', 0, 0, tiled=True)]
    all_gather x1, waiting for transfers between devices: 46.5 us -> 0.02 us  [per_device(): gathered = lax.all_gather(packed, 'seq', axis=0, tiled=False)]
    dot_general x1, matrix products: 9.11 us -> 5.41 us  [per_device(): jnp.einsum('tk,sck->tsc', both, gathered, preferred_element_type=jnp.floa...]
    slice x2, local copies, waits for them, and re-layouts: 0.31 us -> 2.67 us  [per_device(): text_key = keyval[:, :attn].reshape(text_len, heads, HEAD_DIM)]
  transfers between devices with their start and end apart: 3 -> 3, of which waited for: 3 -> 2; matrix products, arithmetic and copies ran while one was open for 9% -> 8% of each run, Pallas kernels for 0% -> 0%
where the time goes in v4:
time: 234 us; the launch traced here: 233 us
  waiting for transfers between devices  143 us (61%)
  local copies, waits for them, and re-layouts  36.2 us (15%)
  starting transfers between devices  16.4 us (7%)
  between operations  14.6 us (6%)
  matrix products  13.7 us (6%)
  other arithmetic  8.97 us (4%)
    all_to_all x1, waiting for transfers between devices, per_device(): recv = lax.all_to_all(send, 'seq', 0, 0, tiled=True)  133 us
    all_to_all x1, starting transfers between devices, per_device(): recv = lax.all_to_all(send, 'seq', 0, 0, tiled=True)  11.3 us
    all_to_all x1, waiting for transfers between devices, per_device(): recv2 = lax.all_to_all(send2, 'seq', 0, 0, tiled=True)  10.5 us
    unnamed x31, local copies, waits for them, and re-layouts  5.91 us
    dot_general x1, matrix products, per_device(): jnp.einsum('tk,sck->tsc', both, gathered, preferred_element_type=jnp.floa...  5.41 us
    all_to_all x1, starting transfers between devices, per_device(): recv2 = lax.all_to_all(send2, 'seq', 0, 0, tiled=True)  5.03 us
  transfers between devices with their start and end apart: 3, of which 2 were waited for; matrix products, arithmetic and copies ran while one was open for 8% of the time, Pallas kernels for 0%

profile of v4, /device:TPU:1, one launch (start us, length us, event | category | flops | bytes accessed | tf_op | source)
XLA Modules:
  0.0 233.0 jit_solution(11492344823812928011)
XLA Ops:
  6.6 0.9 copy-done
  7.7 1.2 convolution_add_fusion.3
  9.2 0.9 fusion.4
  11.5 0.8 copy-done.6
  12.4 2.1 pad_maximum_fusion
  14.5 11.3 %all-to-all-start = ((bf16[32,52,1152]{2,1,0:T(8,128)(2,1)}), bf16[32,52,1152]{2,1,0:T(8,128)(2,1)}, u32[]{:S(2)}, u32[]{:S(2)}) async-start(bf16[32,52,1152]{2,1,0:T(8,128)(2,1)} %pad_maximum_fusion), calls=%async_computation | async-start | bytes 8257536 | tf_op jit(solution)/shard_map/all_to_all | solution.py:102
  26.5 132.7 %all-to-all-done = bf16[32,52,1152]{2,1,0:T(8,128)(2,1)} async-done(((bf16[32,52,1152]{2,1,0:T(8,128)(2,1)}), bf16[32,52,1152]{2,1,0:T(8,128)(2,1)}, u32[]{:S(2)}, u32[]{:S(2)}) %all-to-all-start) | async-done | bytes 3833888 | tf_op jit(solution)/shard_map/all_to_all | solution.py:102
  159.1 1.3 slice_bitcast_fusion
  160.5 5.4 %convolution_convert_fusion.1 = bf16[264,32,112]{2,0,1:T(8,128)(2,1)S(1)} fusion(bf16[32,112,1152]{2,1,0:T(8,128)(2,1)} %bitcast.73, bf16[8,1152]{1,0:T(8,128)(2,1)S(1)} %dynamic-slice_bitcast_fusion, bf16[256,1152]{1,0:T(8,128)(2,1)S(1)} %get-tuple-element.10), kind=kOutput, calls=%fused_computation.15 | convolution fusion | flops 2182152192 | bytes 10758144 | tf_op jit(solution)/shard_map/tk,sck->tsc/dot_general | solution.py:110
  166.5 2.7 %copy.38 = bf16[256,32,54]{2,1,0:T(8,128)(2,1)} copy(bf16[256,32,54]{2,0,1:T(8,128)(2,1)S(1)} %slice.103) | data formatting | bytes 1769472 | tf_op jit(solution)/shard_map/slice | solution.py:112
  169.3 4.2 %convert_element_type.66 = bf16[32,8,1728]{2,1,0:T(8,128)(2,1)S(1)} reshape(bf16[256,32,54]{2,1,0:T(8,128)(2,1)} %copy.38) | data formatting | bytes 1769472 | tf_op jit(solution)/shard_map/convert_element_type | solution.py:112
  175.0 0.7 add_rsqrt_fusion.1
  175.7 1.3 reshape.135
  177.9 1.6 multiply_convert_fusion
  179.5 0.9 fusion.48
  180.5 0.7 fusion.10
  182.7 1.3 reduce.10
  184.1 1.1 reshape.161
  185.2 5.0 %all-to-all-start.1 = ((bf16[32,2,6912]{2,1,0:T(2,128)(2,1)}), bf16[32,2,6912]{2,1,0:T(2,128)(2,1)S(1)}, u32[]{:S(2)}, u32[]{:S(2)}) async-start(bf16[32,2,6912]{2,1,0:T(2,128)(2,1)} %reshape.161), calls=%async_computation.1 | async-start | bytes 1769472 | tf_op jit(solution)/shard_map/all_to_all | solution.py:127
  191.5 4.1 %fusion.46 = (bf16[32,36,576]{2,1,0:T(8,128)(2,1)}, bf16[32,36,576]{2,1,0:T(8,128)(2,1)S(1)}) fusion(bf16[32,52,1152]{2,1,0:T(8,128)(2,1)} %all-to-all-done), kind=kLoop, calls=%fused_computation.92 | loop fusion | bytes 5308416 | tf_op jit(solution)/shard_map/slice | solution.py:132
  195.6 3.6 %reshape.146 = bf16[1152,576]{1,0:T(8,128)(2,1)} reshape(bf16[32,36,576]{2,1,0:T(8,128)(2,1)} %get-tuple-element.8) | data formatting | bytes 2654208 | tf_op jit(solution)/shard_map/reshape | solution.py:132
  199.2 1.5 reshape.141
  200.7 3.4 %slice.115 = bf16[32,18,1152]{2,1,0:T(8,128)(2,1)} slice(bf16[32,112,1152]{2,1,0:T(8,128)(2,1)} %bitcast.74), slice={[0:32], [90:108], [0:1152]} | slice | bytes 2654208 | tf_op jit(solution)/shard_map/slice | solution.py:89
  204.2 10.5 %all-to-all-done.1 = bf16[32,2,6912]{2,1,0:T(2,128)(2,1)S(1)} async-done(((bf16[32,2,6912]{2,1,0:T(2,128)(2,1)}), bf16[32,2,6912]{2,1,0:T(2,128)(2,1)S(1)}, u32[]{:S(2)}, u32[]{:S(2)}) %all-to-all-start.1) | async-done | bytes 884768 | tf_op jit(solution)/shard_map/all_to_all | solution.py:127
  214.6 0.7 reshape.162
  216.1 0.8 fusion.47
  216.9 1.8 copy.47
  218.7 0.9 copy.46
  219.6 0.7 fusion.2
  220.3 0.8 copy-done.4
  223.8 0.9 copy-done.2
  224.6 1.5 fusion.3
  (79 shorter events, 10.9 us)
Async XLA Ops:
  6.5 0.9 copy-start
  6.5 2.4 %copy-start.9 = (bf16[1152,18]{0,1:T(8,128)(2,1)S(1)}, bf16[1152,18]{0,1:T(8,128)(2,1)}, u32[]{:S(2)}) copy-start(bf16[1152,18]{0,1:T(8,128)(2,1)} %param.14) | copy-start | bytes 124420
  6.5 154.0 %all-gather.3.cloned.1.call-start = ((), (), s32[]{:S(2)}) async-start(), calls=%async_computation.2 | async-start | bytes 8515584 | tf_op jit(solution)/shard_map/all_gather | solution.py:86
  7.7 2.5 %copy-start.1 = (bf16[1,256,1152]{2,1,0:T(8,128)(2,1)S(1)}, bf16[1,256,1152]{2,1,0:T(8,128)(2,1)}, u32[]{:S(2)}) copy-start(bf16[1,256,1152]{2,1,0:T(8,128)(2,1)} %param.10) | copy-start | bytes 1769476
  8.9 1.8 copy-start.12
  8.9 1.8 copy-start.10
  8.9 1.8 copy-start.11
  11.3 1.1 copy-start.6
  14.5 144.7 %all-to-all-start = ((bf16[32,52,1152]{2,1,0:T(8,128)(2,1)}), bf16[32,52,1152]{2,1,0:T(8,128)(2,1)}, u32[]{:S(2)}, u32[]{:S(2)}) async-start(bf16[32,52,1152]{2,1,0:T(8,128)(2,1)} %pad_maximum_fusion), calls=%async_computation | async-start | bytes 8257536 | tf_op jit(solution)/shard_map/all_to_all | solution.py:102
  179.5 1.0 copy-start.7
  184.1 6.2 %copy-start.13 = (s32[32]{0:T(128)S(1)}, s32[32]{0:T(128)}, u32[]{:S(2)}) copy-start(s32[32]{0:T(128)} %param.19) | copy-start | bytes 388
  185.2 29.4 %all-to-all-start.1 = ((bf16[32,2,6912]{2,1,0:T(2,128)(2,1)}), bf16[32,2,6912]{2,1,0:T(2,128)(2,1)S(1)}, u32[]{:S(2)}, u32[]{:S(2)}) async-start(bf16[32,2,6912]{2,1,0:T(2,128)(2,1)} %reshape.161), calls=%async_computation.1 | async-start | bytes 1769472 | tf_op jit(solution)/shard_map/all_to_all | solution.py:127
  215.8 3.8 %copy-start.3 = (bf16[1152,576]{1,0:T(8,128)(2,1)S(1)}, bf16[1152,576]{1,0:T(8,128)(2,1)}, u32[]{:S(2)}) copy-start(bf16[1152,576]{1,0:T(8,128)(2,1)} %reshape.141) | copy-start | bytes 3981316
  219.6 1.5 copy-start.4
  221.7 1.0 copy-start.5
  222.2 1.0 copy-start.8
  223.3 1.4 copy-start.2
Sparse Core Ops, SparseCore 0:
  10.3 149.5 all-gather.2

commit v5 on v3

--- a/solution.py
+++ b/solution.py
@@ -80,14 +80,14 @@
     txt_dev = text_len // count
 
     outs_pair = jnp.concatenate([self_out, cross_out], axis=0)
-    sizes = (self_proj.shape[1], cross_keyval.shape[1], cross_query.shape[1], outs_pair.shape[1])
-    packed = pack_rows([self_proj, cross_keyval, cross_query, outs_pair])
+    sizes = (self_proj.shape[1], cross_query.shape[1], outs_pair.shape[1])
+    pad = -sum(sizes) % 16
+    packed = pack_rows([self_proj, cross_query, outs_pair, jnp.zeros((width, pad), self_proj.dtype)])
     gathered = lax.all_gather(packed, "seq", axis=0, tiled=False)
-    kv_at = sizes[0]
-    q_at = kv_at + sizes[1]
-    outs_at = q_at + sizes[2]
-    query_g = gathered[:, q_at : q_at + sizes[2], :]
-    outs_g = gathered[:, outs_at : outs_at + sizes[3], :]
+    q_at = sizes[0]
+    outs_at = q_at + sizes[1]
+    query_g = gathered[:, q_at : q_at + sizes[1], :]
+    outs_g = gathered[:, outs_at : outs_at + sizes[2], :]
 
     tokens = frames_in.astype(jnp.float32)
     normed = (layer_norm(tokens) * (1.0 + modulation[1]) + modulation[0]).astype(jnp.bfloat16)
@@ -103,35 +103,33 @@
     pick = prompt_pick[0]
     memory_rows = lax.dynamic_index_in_dim(recv[:, pix_dev:, :], pick, 0, keepdims=False)
 
+    spread = jnp.broadcast_to(memory_rows[None], (count,) + memory_rows.shape)
+    memory = lax.all_to_all(spread, "seq", 0, 0, tiled=True).reshape(text_len, width)
+    kv_cols = jnp.dot(memory, cross_keyval, preferred_element_type=jnp.float32).astype(jnp.bfloat16)
+
     flat_pix = switched.reshape(-1, width)
-    both = jnp.concatenate([flat_pix, memory_rows], axis=0)
-    both_out = jnp.einsum("tk,sck->tsc", both, gathered, preferred_element_type=jnp.float32)
-    tok = flat_pix.shape[0]
-    qkv = both_out[:tok, :, : sizes[0]].reshape(tok, -1).astype(jnp.bfloat16)
+    qkv_all = jnp.einsum("tk,sck->tsc", flat_pix, gathered, preferred_element_type=jnp.float32)
+    qkv = qkv_all[:, :, : sizes[0]].reshape(flat_pix.shape[0], -1).astype(jnp.bfloat16)
     qkv = qkv.reshape(frames, pix_dev, 3 * attn)
     attended = temporal_attention(qkv, heads, attn, scale_q)
-
-    keyval_rows = both_out[tok:, :, kv_at : kv_at + sizes[1]].reshape(txt_dev, -1).astype(jnp.bfloat16)
-    key_rows = head_norm(keyval_rows[:, :attn].astype(jnp.float32), heads).astype(jnp.bfloat16)
-    kv_rows = jnp.concatenate([key_rows.reshape(txt_dev, attn), keyval_rows[:, attn:]], axis=1)
 
     send2 = jnp.concatenate(
         [
             attended.reshape(count, -1),
-            jnp.broadcast_to(kv_rows.reshape(1, -1), (count, txt_dev * 2 * attn)),
+            jnp.broadcast_to(kv_cols.reshape(1, -1), (count, kv_cols.size)),
         ],
         axis=1,
     )
     recv2 = lax.all_to_all(send2, "seq", 0, 0, tiled=True)
     returned = recv2[:, : pix_dev * attn].reshape(pixels, attn)
-    keyval = recv2[:, pix_dev * attn :].reshape(text_len, 2 * attn)
+    keyval = recv2[:, pix_dev * attn :].reshape(count, text_len, -1).transpose(1, 0, 2).reshape(text_len, 2 * attn)
 
     out_self = outs_g[:, :, :attn].reshape(-1, attn)
     out_cross = outs_g[:, :, attn:].reshape(-1, attn)
     self_term = jnp.einsum("ta,ca->tc", returned, out_self, preferred_element_type=jnp.float32)
     after_self = (tokens.reshape(-1, width) + modulation[2] * self_term).astype(jnp.bfloat16)
 
-    text_key = keyval[:, :attn].reshape(text_len, heads, HEAD_DIM)
+    text_key = head_norm(keyval[:, :attn].astype(jnp.float32), heads).astype(jnp.bfloat16)
     text_value = keyval[:, attn:].reshape(text_len, heads, HEAD_DIM)
     slots = jnp.arange(text_lengths.shape[0], dtype=jnp.int32)
     length = jnp.sum(jnp.where(slots == pick, text_lengths, 0))

time: 189 us -> 196 us (1.037)
  blocking collectives: 0 us -> 27.8 us
  waiting for transfers between devices: 93.5 us -> 71.2 us
  local copies, waits for them, and re-layouts: 35.2 us -> 42.1 us
  matrix products: 18.4 us -> 15.3 us
    all_to_all x0 -> x1, blocking collectives: none -> 27.8 us  [per_device(): lax.all_to_all(spread, 'seq', 0, 0, tiled=True).reshape(text_len, width)]
    all_gather x1, waiting for transfers between devices: 46.5 us -> 23.1 us  [per_device(): gathered = lax.all_gather(packed, 'seq', axis=0, tiled=False)]
    reshape x2, local copies, waits for them, and re-layouts: 0.36 us -> 5.77 us  [per_device(): recv2[:, pix_dev * attn:].reshape(count, text_len, -1).transpose(1, 0, 2)]
    dot_general x1 -> x2, matrix products: 9.11 us -> 6.22 us  [the longest x1 5.93 us: per_device(): jnp.einsum('tk,sck->tsc', flat_pix, gathered, preferred_element_type=jnp....]
    unnamed x31 -> x37, local copies, waits for them, and re-layouts: 4.42 us -> 6.16 us
    slice x10 -> x6, local copies, waits for them, and re-layouts: 9.88 us -> 9.19 us  [the longest x2 5.34 us: per_device(): qkv_all[:, :, :sizes[0]].reshape(flat_pix.shape[0], -1).astype(jnp.bfloat16)]
where the time goes in v5:
time: 196 us; the launch traced here: 195 us
  waiting for transfers between devices  71.2 us (36%)
  local copies, waits for them, and re-layouts  42.1 us (21%)
  blocking collectives  27.8 us (14%)
  starting transfers between devices  15.4 us (8%)
  matrix products  15.3 us (8%)
  between operations  14.5 us (7%)
  other arithmetic  9.03 us (5%)
    all_to_all x1, waiting for transfers between devices, per_device(): recv = lax.all_to_all(send, 'seq', 0, 0, tiled=True)  37.8 us
    all_to_all x1, blocking collectives, per_device(): lax.all_to_all(spread, 'seq', 0, 0, tiled=True).reshape(text_len, width)  27.8 us
    all_gather x1, waiting for transfers between devices, per_device(): gathered = lax.all_gather(packed, 'seq', axis=0, tiled=False)  23.1 us
    all_to_all x1, starting transfers between devices, per_device(): recv = lax.all_to_all(send, 'seq', 0, 0, tiled=True)  10.5 us
    all_to_all x1, waiting for transfers between devices, per_device(): recv2 = lax.all_to_all(send2, 'seq', 0, 0, tiled=True)  10.3 us
    unnamed x37, local copies, waits for them, and re-layouts  6.16 us
    dot_general x1, matrix products, per_device(): jnp.einsum('tk,sck->tsc', flat_pix, gathered, preferred_element_type=jnp....  5.93 us
    reshape x2, local copies, waits for them, and re-layouts, per_device(): recv2[:, pix_dev * attn:].reshape(count, text_len, -1).transpose(1, 0, 2)  5.77 us
  transfers between devices with their start and end apart: 3, of which 3 were waited for; matrix products, arithmetic and copies ran while one was open for 9% of the time, Pallas kernels for 0%

profile of v5, /device:TPU:1, one launch (start us, length us, event | category | flops | bytes accessed | tf_op | source)
XLA Modules:
  0.0 195.4 jit_solution(8277324379752910996)
XLA Ops:
  6.6 0.9 copy-done
  7.7 1.1 convolution_add_fusion.3
  9.1 0.9 fusion.4
  11.1 1.2 pad_maximum_fusion
  12.3 10.5 %all-to-all-start = ((bf16[32,16,1152]{2,1,0:T(8,128)(2,1)}), bf16[32,16,1152]{2,1,0:T(8,128)(2,1)S(1)}, u32[]{:S(2)}, u32[]{:S(2)}) async-start(bf16[32,16,1152]{2,1,0:T(8,128)(2,1)} %pad_maximum_fusion), calls=%async_computation | async-start | bytes 2359296 | tf_op jit(solution)/shard_map/all_to_all | solution.py:101
  23.5 37.8 %all-to-all-done = bf16[32,16,1152]{2,1,0:T(8,128)(2,1)S(1)} async-done(((bf16[32,16,1152]{2,1,0:T(8,128)(2,1)}), bf16[32,16,1152]{2,1,0:T(8,128)(2,1)S(1)}, u32[]{:S(2)}, u32[]{:S(2)}) %all-to-all-start) | async-done | bytes 1179680 | tf_op jit(solution)/shard_map/all_to_all | solution.py:101
  61.4 27.8 %all_to_all.22 = bf16[32,8,1152]{2,1,0:T(8,128)(2,1)S(1)} all-to-all(bf16[32,8,1152]{2,1,0:T(8,128)(2,1)S(1)} %broadcast_in_dim.41), channel_id=1, replica_groups=mesh['clip'=16,'seq'=32] {'seq'}, dimensions={0} | all-to-all | bytes 1179648 | tf_op jit(solution)/shard_map/all_to_all | solution.py:107
  89.9 23.1 %all-gather.3.cloned.1.call-done = bf16[3584,1152]{1,0:T(8,128)(2,1)} async-done(((bf16[112,1152]{1,0:T(8,128)(2,1)}), bf16[3584,1152]{1,0:T(8,128)(2,1)}) %all-gather.3.cloned.1.call-update) | async-done | bytes 8257552 | tf_op jit(solution)/shard_map/all_gather | solution.py:86
  113.0 5.9 %fusion.22 = bf16[256,32,112]{0,2,1:T(8,128)(2,1)S(1)} fusion(bf16[32,112,1152]{2,1,0:T(8,128)(2,1)} %bitcast.78, bf16[32,16,1152]{2,1,0:T(8,128)(2,1)S(1)} %all-to-all-done), kind=kOutput, calls=%fused_computation.48 | convolution fusion | flops 2113929216 | bytes 10682368 | tf_op jit(solution)/shard_map/tk,sck->tsc/dot_general | solution.py:111
  118.9 1.0 slice.117
  119.9 4.3 %copy.36 = bf16[256,32,54]{2,1,0:T(8,128)(2,1)S(1)} copy(bf16[256,32,54]{0,2,1:T(8,128)(2,1)} %slice.117) | data formatting | bytes 1769472 | tf_op jit(solution)/shard_map/slice | solution.py:112
  124.2 4.6 %convert_element_type.57 = bf16[32,8,1728]{2,1,0:T(8,128)(2,1)} reshape(bf16[256,32,54]{2,1,0:T(8,128)(2,1)S(1)} %copy.36) | data formatting | bytes 1769472 | tf_op jit(solution)/shard_map/convert_element_type | solution.py:112
  128.8 2.1 %slice_convert_fusion.2 = (f32[32,8,576]{2,1,0:T(8,128)S(1)}, f32[32,8,576]{2,1,0:T(8,128)S(1)}, bf16[32,8,576]{2,1,0:T(8,128)(2,1)}) fusion(bf16[32,8,1728]{2,1,0:T(8,128)(2,1)} %convert_element_type.57), kind=kLoop, calls=%fused_computation.58 | loop fusion | flops 294912 | bytes 2359296 | tf_op jit(solution)/shard_map/reshape | solution.py:22
  133.9 1.3 reshape.137
  136.0 0.9 fusion.50
  139.2 1.3 reduce.10
  140.5 1.1 reshape.168
  141.7 4.9 %all-to-all-start.2 = ((bf16[32,2,6912]{2,1,0:T(2,128)(2,1)}), bf16[32,2,6912]{2,1,0:T(2,128)(2,1)S(1)}, u32[]{:S(2)}, u32[]{:S(2)}) async-start(bf16[32,2,6912]{2,1,0:T(2,128)(2,1)} %reshape.168), calls=%async_computation.2 | async-start | bytes 1769472 | tf_op jit(solution)/shard_map/all_to_all | solution.py:123
  147.9 3.7 %slice.99 = bf16[32,18,1152]{2,1,0:T(8,128)(2,1)} slice(bf16[32,112,1152]{2,1,0:T(8,128)(2,1)} %bitcast.79), slice={[0:32], [54:72], [0:1152]} | slice | bytes 2654208 | tf_op jit(solution)/shard_map/slice | solution.py:89
  151.6 4.0 %fusion.48 = (bf16[32,36,576]{2,1,0:T(8,128)(2,1)S(1)}, bf16[32,36,576]{2,1,0:T(8,128)(2,1)}) fusion(bf16[32,112,1152]{2,1,0:T(8,128)(2,1)} %bitcast.80), kind=kLoop, calls=%fused_computation.90 | loop fusion | bytes 5308416 | tf_op jit(solution)/shard_map/slice | solution.py:128
  155.6 3.5 %reshape.144 = bf16[1152,576]{1,0:T(8,128)(2,1)} reshape(bf16[32,36,576]{2,1,0:T(8,128)(2,1)} %get-tuple-element.9) | data formatting | bytes 2654208 | tf_op jit(solution)/shard_map/reshape | solution.py:127
  159.2 1.5 reshape.151
  160.7 10.3 %all-to-all-done.2 = bf16[32,2,6912]{2,1,0:T(2,128)(2,1)S(1)} async-done(((bf16[32,2,6912]{2,1,0:T(2,128)(2,1)}), bf16[32,2,6912]{2,1,0:T(2,128)(2,1)S(1)}, u32[]{:S(2)}, u32[]{:S(2)}) %all-to-all-start.2) | async-done | bytes 884768 | tf_op jit(solution)/shard_map/all_to_all | solution.py:123
  171.0 0.7 reshape.169
  171.9 1.0 reshape.143
  173.3 1.8 fusion.2
  176.3 0.9 reshape_reshape.7
  177.2 5.7 %reshape.145 = bf16[32,256,36]{2,1,0:T(8,128)(2,1)S(1)} reshape(bf16[32,9216]{1,0:T(8,128)(2,1)S(1)} %slice.96) | data formatting | bytes 1179648 | tf_op jit(solution)/shard_map/reshape | solution.py:125
  182.9 1.0 copy.44
  184.1 0.8 copy-done.4
  186.0 0.9 copy-done.2
  187.0 1.5 fusion.3
  (77 shorter events, 12.7 us)
Async XLA Ops:
  6.5 0.9 copy-start
  6.5 2.3 %copy-start.14 = (bf16[576,36]{0,1:T(8,128)(2,1)S(1)}, bf16[576,36]{0,1:T(8,128)(2,1)}, u32[]{:S(2)}) copy-start(bf16[576,36]{0,1:T(8,128)(2,1)} %param.13) | copy-start | bytes 124420
  6.5 2.3 %copy-start.13 = (bf16[576,36]{0,1:T(8,128)(2,1)S(1)}, bf16[576,36]{0,1:T(8,128)(2,1)}, u32[]{:S(2)}) copy-start(bf16[576,36]{0,1:T(8,128)(2,1)} %param.16) | copy-start | bytes 124420
  6.5 106.4 %all-gather.3.cloned.1.call-start = ((), (), s32[]{:S(2)}) async-start(), calls=%async_computation.3 | async-start | bytes 8515584 | tf_op jit(solution)/shard_map/all_gather | solution.py:86
  7.7 2.4 %copy-start.15 = (f32[3,1152]{1,0:T(4,128)S(1)}, f32[3,1152]{1,0:T(4,128)}, u32[]{:S(2)}) copy-start(f32[3,1152]{1,0:T(4,128)} %param.11) | copy-start | bytes 41476
  7.7 2.5 %copy-start.1 = (bf16[1,256,1152]{2,1,0:T(8,128)(2,1)S(1)}, bf16[1,256,1152]{2,1,0:T(8,128)(2,1)}, u32[]{:S(2)}) copy-start(bf16[1,256,1152]{2,1,0:T(8,128)(2,1)} %param.10) | copy-start | bytes 1769476
  10.1 1.1 copy-start.9
  12.3 49.0 %all-to-all-start = ((bf16[32,16,1152]{2,1,0:T(8,128)(2,1)}), bf16[32,16,1152]{2,1,0:T(8,128)(2,1)S(1)}, u32[]{:S(2)}, u32[]{:S(2)}) async-start(bf16[32,16,1152]{2,1,0:T(8,128)(2,1)} %pad_maximum_fusion), calls=%async_computation | async-start | bytes 2359296 | tf_op jit(solution)/shard_map/all_to_all | solution.py:101
  23.5 65.8 %copy-start.12 = (bf16[1152,36]{0,1:T(8,128)(2,1)S(1)}, bf16[1152,36]{0,1:T(8,128)(2,1)}, u32[]{:S(2)}) copy-start(bf16[1152,36]{0,1:T(8,128)(2,1)} %param.15) | copy-start | bytes 248836
  132.9 1.0 copy-start.8
  133.0 2.3 %copy-start.11 = (f32[32,8,8]{2,1,0:T(8,128)S(1)}, f32[32,8,8]{2,1,0:T(8,128)}, u32[]{:S(2)}) copy-start(f32[32,8,8]{2,1,0:T(8,128)} %add_rsqrt_fusion) | copy-start | bytes 24580
  136.0 1.0 copy-start.10
  140.5 6.1 %copy-start.16 = (s32[32]{0:T(128)S(1)}, s32[32]{0:T(128)}, u32[]{:S(2)}) copy-start(s32[32]{0:T(128)} %param.19) | copy-start | bytes 388
  141.7 29.3 %all-to-all-start.2 = ((bf16[32,2,6912]{2,1,0:T(2,128)(2,1)}), bf16[32,2,6912]{2,1,0:T(2,128)(2,1)S(1)}, u32[]{:S(2)}, u32[]{:S(2)}) async-start(bf16[32,2,6912]{2,1,0:T(2,128)(2,1)} %reshape.168), calls=%async_computation.2 | async-start | bytes 1769472 | tf_op jit(solution)/shard_map/all_to_all | solution.py:123
  171.8 1.5 copy-start.3
  173.3 1.8 copy-start.7
  175.1 0.8 copy-start.5
  183.9 1.1 copy-start.4
  185.5 1.4 copy-start.2
  185.5 1.5 copy-start.6
Sparse Core Ops, SparseCore 0:
  10.2 102.6 all-gather.2

commit v6 on v3

--- a/solution.py
+++ b/solution.py
@@ -24,18 +24,20 @@
     return shaped * lax.rsqrt(power + EPS)
 
 
-def temporal_attention(qkv, heads, attn, scale_q):
-    frames, patches = (qkv.shape[0], qkv.shape[1])
-    query = (head_norm(qkv[..., :attn].astype(jnp.float32), heads) * scale_q).astype(jnp.bfloat16)
-    key = head_norm(qkv[..., attn : 2 * attn].astype(jnp.float32), heads).astype(jnp.bfloat16)
-    value = qkv[..., 2 * attn :].reshape(frames, patches, heads, attn // heads)
-    scores = jnp.einsum("fphd,gphd->phfg", query, key, preferred_element_type=jnp.float32)
-    weights = jnp.exp(scores)
+def temporal_attention(qkv, heads, attn, scale_q, patches):
+    tokens = qkv.shape[0]
+    query = (head_norm(qkv[:, :attn].astype(jnp.float32), heads) * scale_q).astype(jnp.bfloat16)
+    key = head_norm(qkv[:, attn : 2 * attn].astype(jnp.float32), heads).astype(jnp.bfloat16)
+    value = qkv[:, 2 * attn :].reshape(tokens, heads, attn // heads)
+    scores = jnp.einsum("thd,uhd->htu", query, key, preferred_element_type=jnp.float32)
+    patch = jnp.arange(tokens, dtype=jnp.int32) % patches
+    same = patch[:, None] == patch[None, :]
+    weights = jnp.where(same, jnp.exp(scores), 0.0)
     total = jnp.sum(weights, axis=-1)
     probs = weights.astype(jnp.bfloat16)
-    mixed = jnp.einsum("phfg,gphd->fphd", probs, value, preferred_element_type=jnp.float32)
-    attended = mixed / jnp.transpose(total, (2, 0, 1))[..., None]
-    return attended.astype(jnp.bfloat16).reshape(frames, patches, attn)
+    mixed = jnp.einsum("htu,uhd->thd", probs, value, preferred_element_type=jnp.float32)
+    attended = mixed / jnp.transpose(total)[..., None]
+    return attended.astype(jnp.bfloat16).reshape(tokens, attn)
 
 
 def pack_rows(pieces):
@@ -108,8 +110,7 @@
     both_out = jnp.einsum("tk,sck->tsc", both, gathered, preferred_element_type=jnp.float32)
     tok = flat_pix.shape[0]
     qkv = both_out[:tok, :, : sizes[0]].reshape(tok, -1).astype(jnp.bfloat16)
-    qkv = qkv.reshape(frames, pix_dev, 3 * attn)
-    attended = temporal_attention(qkv, heads, attn, scale_q)
+    attended = temporal_attention(qkv, heads, attn, scale_q, pix_dev)
 
     keyval_rows = both_out[tok:, :, kv_at : kv_at + sizes[1]].reshape(txt_dev, -1).astype(jnp.bfloat16)
     key_rows = head_norm(keyval_rows[:, :attn].astype(jnp.float32), heads).astype(jnp.bfloat16)

time: 189 us -> 172 us (0.910)
  local copies, waits for them, and re-layouts: 35.2 us -> 25.7 us
  other arithmetic: 10.7 us -> 5.14 us
    slice x2 -> x1, local copies, waits for them, and re-layouts: 5.29 us -> 0.06 us  [per_device(): qkv = both_out[:tok, :, :sizes[0]].reshape(tok, -1).astype(jnp.bfloat16)]
    convert_element_type x1, local copies, waits for them, and re-layouts: 4.57 us -> 0.23 us  [per_device(): qkv = both_out[:tok, :, :sizes[0]].reshape(tok, -1).astype(jnp.bfloat16)]
    reshape x3 -> x0, local copies, waits for them, and re-layouts: 2.3 us -> none  [the longest x1 1.35 us: temporal_attention(): value = qkv[..., 2 * attn:].reshape(frames, patches, heads, attn // heads)]
    reshape x1 -> x0, other arithmetic: 2.09 us -> none  [head_norm(): values.reshape(values.shape[:-1] + (heads, values.shape[-1] // heads))]
    unnamed x31 -> x27, local copies, waits for them, and re-layouts: 4.42 us -> 4.91 us
  transfers between devices with their start and end apart: 3 -> 3, of which waited for: 3 -> 3; matrix products, arithmetic and copies ran while one was open for 9% -> 10% of each run, Pallas kernels for 0% -> 0%
where the time goes in v6:
time: 172 us; the launch traced here: 171 us
  waiting for transfers between devices  93.2 us (54%)
  local copies, waits for them, and re-layouts  25.7 us (15%)
  matrix products  16.8 us (10%)
  starting transfers between devices  16 us (9%)
  between operations  14.5 us (8%)
  other arithmetic  5.14 us (3%)
    all_gather x1, waiting for transfers between devices, per_device(): gathered = lax.all_gather(packed, 'seq', axis=0, tiled=False)  46.4 us
    all_to_all x1, waiting for transfers between devices, per_device(): recv = lax.all_to_all(send, 'seq', 0, 0, tiled=True)  37.7 us
    all_to_all x1, starting transfers between devices, per_device(): recv = lax.all_to_all(send, 'seq', 0, 0, tiled=True)  10.5 us
    all_to_all x1, waiting for transfers between devices, per_device(): recv2 = lax.all_to_all(send2, 'seq', 0, 0, tiled=True)  9.14 us
    dot_general x1, matrix products, per_device(): jnp.einsum('tk,sck->tsc', both, gathered, preferred_element_type=jnp.floa...  9.11 us
    all_to_all x1, starting transfers between devices, per_device(): recv2 = lax.all_to_all(send2, 'seq', 0, 0, tiled=True)  5.49 us
    slice x1, local copies, waits for them, and re-layouts, per_device(): out_cross = outs_g[:, :, attn:].reshape(-1, attn)  5.28 us
    unnamed x27, local copies, waits for them, and re-layouts  4.91 us
  transfers between devices with their start and end apart: 3, of which 3 were waited for; matrix products, arithmetic and copies ran while one was open for 10% of the time, Pallas kernels for 0%

profile of v6, /device:TPU:1, one launch (start us, length us, event | category | flops | bytes accessed | tf_op | source)
XLA Modules:
  0.0 171.3 jit_solution(17400219844392284938)
XLA Ops:
  6.6 0.9 copy-done
  7.7 1.2 convolution_add_fusion.3
  9.2 1.0 fusion.4
  11.3 1.1 pad_maximum_fusion
  12.4 10.5 %all-to-all-start = ((bf16[32,16,1152]{2,1,0:T(8,128)(2,1)}), bf16[32,16,1152]{2,1,0:T(8,128)(2,1)S(1)}, u32[]{:S(2)}, u32[]{:S(2)}) async-start(bf16[32,16,1152]{2,1,0:T(8,128)(2,1)} %pad_maximum_fusion), calls=%async_computation | async-start | bytes 2359296 | tf_op jit(solution)/shard_map/all_to_all | solution.py:103
  23.7 37.7 %all-to-all-done = bf16[32,16,1152]{2,1,0:T(8,128)(2,1)S(1)} async-done(((bf16[32,16,1152]{2,1,0:T(8,128)(2,1)}), bf16[32,16,1152]{2,1,0:T(8,128)(2,1)S(1)}, u32[]{:S(2)}, u32[]{:S(2)}) %all-to-all-start) | async-done | bytes 1179680 | tf_op jit(solution)/shard_map/all_to_all | solution.py:103
  61.5 46.4 %all-gather.3.cloned.1.call-done = bf16[4608,1152]{1,0:T(8,128)(2,1)} async-done(((bf16[144,1152]{1,0:T(8,128)(2,1)}), bf16[4608,1152]{1,0:T(8,128)(2,1)}) %all-gather.3.cloned.1.call-update) | async-done | bytes 10616848 | tf_op jit(solution)/shard_map/all_gather | solution.py:87
  107.8 9.1 %convolution_convert_fusion = bf16[264,32,144]{0,2,1:T(8,128)(2,1)S(1)} fusion(bf16[32,144,1152]{2,1,0:T(8,128)(2,1)} %bitcast.76, bf16[8,1152]{1,0:T(8,128)(2,1)S(1)} %dynamic-slice_bitcast_fusion, bf16[256,1152]{1,0:T(8,128)(2,1)S(1)} %get-tuple-element.10), kind=kOutput, calls=%fused_computation.9 | convolution fusion | flops 2805276672 | bytes 13658112 | tf_op jit(solution)/shard_map/tk,sck->tsc/dot_general | solution.py:110
  118.1 0.6 fusion.5
  119.6 0.7 reshape_reshape.6
  120.8 0.5 broadcast.158
  121.3 1.3 reduce.10
  122.7 1.1 reshape.174
  123.8 5.5 %all-to-all-start.1 = ((bf16[32,2,6912]{2,1,0:T(2,128)(2,1)}), bf16[32,2,6912]{2,1,0:T(2,128)(2,1)S(1)}, u32[]{:S(2)}, u32[]{:S(2)}) async-start(bf16[32,2,6912]{2,1,0:T(2,128)(2,1)} %reshape.174), calls=%async_computation.1 | async-start | bytes 1769472 | tf_op jit(solution)/shard_map/all_to_all | solution.py:126
  129.3 0.6 fusion.51
  129.9 0.6 iota_compare_fusion.1
  130.6 3.6 %slice.115 = bf16[32,18,1152]{2,1,0:T(8,128)(2,1)} slice(bf16[32,144,1152]{2,1,0:T(8,128)(2,1)} %bitcast.77), slice={[0:32], [90:108], [0:1152]} | slice | bytes 2654208 | tf_op jit(solution)/shard_map/slice | solution.py:91
  134.2 5.3 %fusion.58 = (bf16[32,36,576]{2,1,0:T(8,128)(2,1)S(1)}, bf16[32,36,576]{2,1,0:T(8,128)(2,1)}) fusion(bf16[32,144,1152]{2,1,0:T(8,128)(2,1)} %bitcast.78), kind=kLoop, calls=%fused_computation.99 | loop fusion | bytes 5308416 | tf_op jit(solution)/shard_map/slice | solution.py:131
  139.5 3.5 %reshape.156 = bf16[1152,576]{1,0:T(8,128)(2,1)} reshape(bf16[32,36,576]{2,1,0:T(8,128)(2,1)} %get-tuple-element.9) | data formatting | bytes 2654208 | tf_op jit(solution)/shard_map/reshape | solution.py:130
  143.0 1.5 reshape.161
  144.5 9.1 %all-to-all-done.1 = bf16[32,2,6912]{2,1,0:T(2,128)(2,1)S(1)} async-done(((bf16[32,2,6912]{2,1,0:T(2,128)(2,1)}), bf16[32,2,6912]{2,1,0:T(2,128)(2,1)S(1)}, u32[]{:S(2)}, u32[]{:S(2)}) %all-to-all-start.1) | async-done | bytes 884768 | tf_op jit(solution)/shard_map/all_to_all | solution.py:126
  153.7 0.7 reshape.175
  154.5 0.7 slice.110
  155.7 0.9 copy.34
  156.8 1.2 reshape.155
  158.0 0.7 fusion.2
  158.7 0.8 copy-done.4
  159.5 0.6 multiply_reduce_fusion
  160.6 0.7 bitcast_reduce_fusion
  161.5 0.5 fusion.14
  162.0 0.9 copy-done.2
  162.9 1.5 fusion.3
  (69 shorter events, 5.7 us)
Async XLA Ops:
  6.5 0.9 copy-start
  6.5 2.3 %copy-start.7 = (bf16[1152,18]{0,1:T(8,128)(2,1)S(1)}, bf16[1152,18]{0,1:T(8,128)(2,1)}, u32[]{:S(2)}) copy-start(bf16[1152,18]{0,1:T(8,128)(2,1)} %param.14) | copy-start | bytes 124420
  6.5 101.3 %all-gather.3.cloned.1.call-start = ((), (), s32[]{:S(2)}) async-start(), calls=%async_computation.2 | async-start | bytes 10948608 | tf_op jit(solution)/shard_map/all_gather | solution.py:87
  7.4 1.8 %copy-start.8 = (bf16[576,36]{0,1:T(8,128)(2,1)S(1)}, bf16[576,36]{0,1:T(8,128)(2,1)}, u32[]{:S(2)}) copy-start(bf16[576,36]{0,1:T(8,128)(2,1)} %param.16) | copy-start | bytes 124420
  7.4 1.8 %copy-start.9 = (bf16[576,36]{0,1:T(8,128)(2,1)S(1)}, bf16[576,36]{0,1:T(8,128)(2,1)}, u32[]{:S(2)}) copy-start(bf16[576,36]{0,1:T(8,128)(2,1)} %param.13) | copy-start | bytes 124420
  8.9 1.4 copy-start.10
  8.9 1.4 copy-start.1
  10.2 1.1 copy-start.5
  12.4 48.9 %all-to-all-start = ((bf16[32,16,1152]{2,1,0:T(8,128)(2,1)}), bf16[32,16,1152]{2,1,0:T(8,128)(2,1)S(1)}, u32[]{:S(2)}, u32[]{:S(2)}) async-start(bf16[32,16,1152]{2,1,0:T(8,128)(2,1)} %pad_maximum_fusion), calls=%async_computation | async-start | bytes 2359296 | tf_op jit(solution)/shard_map/all_to_all | solution.py:103
  122.7 6.6 %copy-start.11 = (s32[32]{0:T(128)S(1)}, s32[32]{0:T(128)}, u32[]{:S(2)}) copy-start(s32[32]{0:T(128)} %param.19) | copy-start | bytes 388
  123.8 29.9 %all-to-all-start.1 = ((bf16[32,2,6912]{2,1,0:T(2,128)(2,1)}), bf16[32,2,6912]{2,1,0:T(2,128)(2,1)S(1)}, u32[]{:S(2)}, u32[]{:S(2)}) async-start(bf16[32,2,6912]{2,1,0:T(2,128)(2,1)} %reshape.174), calls=%async_computation.1 | async-start | bytes 1769472 | tf_op jit(solution)/shard_map/all_to_all | solution.py:126
  155.6 2.5 %copy-start.3 = (bf16[1152,576]{1,0:T(8,128)(2,1)S(1)}, bf16[1152,576]{1,0:T(8,128)(2,1)}, u32[]{:S(2)}) copy-start(bf16[1152,576]{1,0:T(8,128)(2,1)} %reshape.156) | copy-start | bytes 3981316
  158.0 1.5 copy-start.4
  160.5 1.0 copy-start.6
  161.5 1.4 copy-start.2
Sparse Core Ops, SparseCore 0:
  10.4 97.4 all-gather.2

commit v7 on v6

--- a/solution.py
+++ b/solution.py
@@ -107,7 +107,10 @@
 
     flat_pix = switched.reshape(-1, width)
     both = jnp.concatenate([flat_pix, memory_rows], axis=0)
-    both_out = jnp.einsum("tk,sck->tsc", both, gathered, preferred_element_type=jnp.float32)
+    lead = -(-(kv_at + sizes[1]) // 16) * 16
+    both_out = jnp.einsum(
+        "tk,sck->tsc", both, gathered[:, :lead, :], preferred_element_type=jnp.float32
+    )
     tok = flat_pix.shape[0]
     qkv = both_out[:tok, :, : sizes[0]].reshape(tok, -1).astype(jnp.bfloat16)
     attended = temporal_attention(qkv, heads, attn, scale_q, pix_dev)

time: 172 us -> 172 us (level)
  matrix products: 16.8 us -> 12.9 us
  local copies, waits for them, and re-layouts: 25.7 us -> 28.7 us
    dot_general x1, matrix products: 9.11 us -> 5.24 us  [per_device(): jnp.einsum('tk,sck->tsc', both, gathered[:, :lead, :], preferred_element_...]
    slice x2, local copies, waits for them, and re-layouts: 0.31 us -> 2.69 us  [per_device(): text_key = keyval[:, :attn].reshape(text_len, heads, HEAD_DIM)]
    reshape x1, local copies, waits for them, and re-layouts: 1.52 us -> 3.55 us  [per_device(): out_cross = outs_g[:, :, attn:].reshape(-1, attn)]
    reshape x1, local copies, waits for them, and re-layouts: 3.55 us -> 1.52 us  [per_device(): out_self = outs_g[:, :, :attn].reshape(-1, attn)]
    slice x1 -> x2, local copies, waits for them, and re-layouts: 0.06 us -> 2.01 us  [per_device(): qkv = both_out[:tok, :, :sizes[0]].reshape(tok, -1).astype(jnp.bfloat16)]
    unnamed x27 -> x29, local copies, waits for them, and re-layouts: 4.91 us -> 5.12 us
where the time goes in v7:
time: 172 us; the launch traced here: 171 us
  waiting for transfers between devices  93.9 us (55%)
  local copies, waits for them, and re-layouts  28.7 us (17%)
  starting transfers between devices  16 us (9%)
  between operations  14.5 us (8%)
  matrix products  12.9 us (8%)
  other arithmetic  5.13 us (3%)
    all_gather x1, waiting for transfers between devices, per_device(): gathered = lax.all_gather(packed, 'seq', axis=0, tiled=False)  46.4 us
    all_to_all x1, waiting for transfers between devices, per_device(): recv = lax.all_to_all(send, 'seq', 0, 0, tiled=True)  37.7 us
    all_to_all x1, starting transfers between devices, per_device(): recv = lax.all_to_all(send, 'seq', 0, 0, tiled=True)  10.5 us
    all_to_all x1, waiting for transfers between devices, per_device(): recv2 = lax.all_to_all(send2, 'seq', 0, 0, tiled=True)  9.8 us
    all_to_all x1, starting transfers between devices, per_device(): recv2 = lax.all_to_all(send2, 'seq', 0, 0, tiled=True)  5.5 us
    dot_general x1, matrix products, per_device(): jnp.einsum('tk,sck->tsc', both, gathered[:, :lead, :], preferred_element_...  5.24 us
    unnamed x29, local copies, waits for them, and re-layouts  5.12 us
    slice x1, local copies, waits for them, and re-layouts, per_device(): out_cross = outs_g[:, :, attn:].reshape(-1, attn)  4.62 us
  transfers between devices with their start and end apart: 3, of which 3 were waited for; matrix products, arithmetic and copies ran while one was open for 10% of the time, Pallas kernels for 0%

profile of v7, /device:TPU:1, one launch (start us, length us, event | category | flops | bytes accessed | tf_op | source)
XLA Modules:
  0.0 171.0 jit_solution(11490369639092395571)
XLA Ops:
  6.6 0.9 copy-done
  7.7 1.2 convolution_add_fusion.3
  9.2 1.0 fusion.6
  11.3 1.1 pad_maximum_fusion
  12.4 10.5 %all-to-all-start = ((bf16[32,16,1152]{2,1,0:T(8,128)(2,1)}), bf16[32,16,1152]{2,1,0:T(8,128)(2,1)S(1)}, u32[]{:S(2)}, u32[]{:S(2)}) async-start(bf16[32,16,1152]{2,1,0:T(8,128)(2,1)} %pad_maximum_fusion), calls=%async_computation | async-start | bytes 2359296 | tf_op jit(solution)/shard_map/all_to_all | solution.py:103
  23.7 37.7 %all-to-all-done = bf16[32,16,1152]{2,1,0:T(8,128)(2,1)S(1)} async-done(((bf16[32,16,1152]{2,1,0:T(8,128)(2,1)}), bf16[32,16,1152]{2,1,0:T(8,128)(2,1)S(1)}, u32[]{:S(2)}, u32[]{:S(2)}) %all-to-all-start) | async-done | bytes 1179680 | tf_op jit(solution)/shard_map/all_to_all | solution.py:103
  61.5 46.4 %all-gather.3.cloned.1.call-done = bf16[4608,1152]{1,0:T(8,128)(2,1)} async-done(((bf16[144,1152]{1,0:T(8,128)(2,1)}), bf16[4608,1152]{1,0:T(8,128)(2,1)}) %all-gather.3.cloned.1.call-update) | async-done | bytes 10616848 | tf_op jit(solution)/shard_map/all_gather | solution.py:87
  107.8 5.2 %fusion.7 = bf16[264,32,96]{2,0,1:T(8,128)(2,1)S(1)} fusion(bf16[32,144,1152]{2,1,0:T(8,128)(2,1)} %bitcast.75, bf16[8,1152]{1,0:T(8,128)(2,1)S(1)} %dynamic-slice_bitcast_fusion, bf16[256,1152]{1,0:T(8,128)(2,1)S(1)} %get-tuple-element.10), kind=kOutput, calls=%fused_computation.16 | convolution fusion | flops 1870589952 | bytes 9308160 | tf_op jit(solution)/shard_map/tk,sck->tsc/dot_general | solution.py:111
  113.7 1.8 %copy.32 = bf16[256,32,54]{0,2,1:T(8,128)(2,1)} copy(bf16[256,32,54]{2,0,1:T(8,128)(2,1)S(1)} %slice.108) | data formatting | bytes 1769472 | tf_op jit(solution)/shard_map/slice | solution.py:115
  115.4 1.3 convert_element_type.60
  117.5 0.6 fusion.10
  118.9 0.7 reshape_reshape.6
  120.2 1.3 reduce.10
  121.6 1.1 reshape.174
  122.7 5.5 %all-to-all-start.1 = ((bf16[32,2,6912]{2,1,0:T(2,128)(2,1)}), bf16[32,2,6912]{2,1,0:T(2,128)(2,1)S(1)}, u32[]{:S(2)}, u32[]{:S(2)}) async-start(bf16[32,2,6912]{2,1,0:T(2,128)(2,1)} %reshape.174), calls=%async_computation.1 | async-start | bytes 1769472 | tf_op jit(solution)/shard_map/all_to_all | solution.py:129
  128.2 0.6 fusion.56
  128.8 0.6 iota_compare_fusion.1
  129.5 3.6 %slice.120 = bf16[32,18,1152]{2,1,0:T(8,128)(2,1)} slice(bf16[32,144,1152]{2,1,0:T(8,128)(2,1)} %bitcast.76), slice={[0:32], [90:108], [0:1152]} | slice | bytes 2654208 | tf_op jit(solution)/shard_map/slice | solution.py:91
  133.1 4.6 %fusion.63 = (bf16[32,36,576]{2,1,0:T(8,128)(2,1)}, bf16[32,36,576]{2,1,0:T(8,128)(2,1)S(1)}) fusion(bf16[32,144,1152]{2,1,0:T(8,128)(2,1)} %bitcast.77), kind=kLoop, calls=%fused_computation.101 | loop fusion | bytes 5308416 | tf_op jit(solution)/shard_map/slice | solution.py:134
  137.7 3.5 %reshape.161 = bf16[1152,576]{1,0:T(8,128)(2,1)} reshape(bf16[32,36,576]{2,1,0:T(8,128)(2,1)} %get-tuple-element.8) | data formatting | bytes 2654208 | tf_op jit(solution)/shard_map/reshape | solution.py:134
  141.2 1.5 reshape.156
  142.8 9.8 %all-to-all-done.1 = bf16[32,2,6912]{2,1,0:T(2,128)(2,1)S(1)} async-done(((bf16[32,2,6912]{2,1,0:T(2,128)(2,1)}), bf16[32,2,6912]{2,1,0:T(2,128)(2,1)S(1)}, u32[]{:S(2)}, u32[]{:S(2)}) %all-to-all-start.1) | async-done | bytes 884768 | tf_op jit(solution)/shard_map/all_to_all | solution.py:129
  152.6 0.7 reshape.175
  154.0 0.8 fusion.65
  154.9 1.9 %copy.38 = bf16[256,576]{0,1:T(8,128)(2,1)} copy(bf16[256,576]{1,0:T(8,128)(2,1)} %get-tuple-element.15) | data formatting | bytes 589824 | tf_op jit(solution)/shard_map/slice | solution.py:138
  156.7 0.9 copy.37
  157.6 0.7 fusion.4
  158.3 0.8 copy-done.4
  159.1 0.6 multiply_reduce_fusion
  160.6 0.6 bitcast_reduce_fusion
  161.8 0.9 copy-done.2
  162.7 1.5 fusion.5
  (72 shorter events, 6.5 us)
Async XLA Ops:
  6.5 0.9 copy-start
  6.5 2.3 %copy-start.8 = (bf16[1152,18]{0,1:T(8,128)(2,1)S(1)}, bf16[1152,18]{0,1:T(8,128)(2,1)}, u32[]{:S(2)}) copy-start(bf16[1152,18]{0,1:T(8,128)(2,1)} %param.14) | copy-start | bytes 124420
  6.5 101.3 %all-gather.3.cloned.1.call-start = ((), (), s32[]{:S(2)}) async-start(), calls=%async_computation.2 | async-start | bytes 10948608 | tf_op jit(solution)/shard_map/all_gather | solution.py:87
  7.4 1.8 %copy-start.9 = (bf16[576,36]{0,1:T(8,128)(2,1)S(1)}, bf16[576,36]{0,1:T(8,128)(2,1)}, u32[]{:S(2)}) copy-start(bf16[576,36]{0,1:T(8,128)(2,1)} %param.16) | copy-start | bytes 124420
  7.4 1.8 %copy-start.10 = (bf16[576,36]{0,1:T(8,128)(2,1)S(1)}, bf16[576,36]{0,1:T(8,128)(2,1)}, u32[]{:S(2)}) copy-start(bf16[576,36]{0,1:T(8,128)(2,1)} %param.13) | copy-start | bytes 124420
  8.9 1.4 copy-start.11
  8.9 1.4 copy-start.1
  10.2 1.1 copy-start.6
  12.4 48.9 %all-to-all-start = ((bf16[32,16,1152]{2,1,0:T(8,128)(2,1)}), bf16[32,16,1152]{2,1,0:T(8,128)(2,1)S(1)}, u32[]{:S(2)}, u32[]{:S(2)}) async-start(bf16[32,16,1152]{2,1,0:T(8,128)(2,1)} %pad_maximum_fusion), calls=%async_computation | async-start | bytes 2359296 | tf_op jit(solution)/shard_map/all_to_all | solution.py:103
  121.5 6.6 %copy-start.12 = (s32[32]{0:T(128)S(1)}, s32[32]{0:T(128)}, u32[]{:S(2)}) copy-start(s32[32]{0:T(128)} %param.19) | copy-start | bytes 388
  122.7 29.9 %all-to-all-start.1 = ((bf16[32,2,6912]{2,1,0:T(2,128)(2,1)}), bf16[32,2,6912]{2,1,0:T(2,128)(2,1)S(1)}, u32[]{:S(2)}, u32[]{:S(2)}) async-start(bf16[32,2,6912]{2,1,0:T(2,128)(2,1)} %reshape.174), calls=%async_computation.1 | async-start | bytes 1769472 | tf_op jit(solution)/shard_map/all_to_all | solution.py:129
  153.7 3.9 %copy-start.3 = (bf16[1152,576]{1,0:T(8,128)(2,1)S(1)}, bf16[1152,576]{1,0:T(8,128)(2,1)}, u32[]{:S(2)}) copy-start(bf16[1152,576]{1,0:T(8,128)(2,1)} %reshape.156) | copy-start | bytes 3981316
  157.6 1.5 copy-start.4
  159.7 1.0 copy-start.5
  160.2 1.1 copy-start.7
  161.3 1.4 copy-start.2
Sparse Core Ops, SparseCore 0:
  10.4 97.4 all-gather.2

commit v8 on v7

--- a/solution.py
+++ b/solution.py
@@ -41,16 +41,9 @@
 
 
 def pack_rows(pieces):
-    total = sum(p.shape[1] for p in pieces)
-    eye = jnp.eye(total, dtype=pieces[0].dtype)
-    packed, start = None, 0
-    for p in pieces:
-        part = jnp.einsum(
-            "rc,kc->rk", eye[:, start : start + p.shape[1]], p, preferred_element_type=jnp.float32
-        )
-        packed = part if packed is None else packed + part
-        start += p.shape[1]
-    return packed.astype(pieces[0].dtype)
+    joined = jnp.concatenate(pieces, axis=1)
+    eye = jnp.eye(joined.shape[1], dtype=joined.dtype)
+    return jnp.einsum("rc,kc->rk", eye, joined, preferred_element_type=joined.dtype)
 
 
 def project(x, gathered):

time: 172 us -> 170 us (0.988)
    unnamed x29 -> x21, local copies, waits for them, and re-layouts: 5.12 us -> 4.22 us
where the time goes in v8:
time: 170 us
  waiting for transfers between devices  94.2 us (55%)
  local copies, waits for them, and re-layouts  27.8 us (16%)
  starting transfers between devices  15.8 us (9%)
  between operations  14.4 us (8%)
  matrix products  12.3 us (7%)
  other arithmetic  5.12 us (3%)
    all_gather x1, waiting for transfers between devices, per_device(): gathered = lax.all_gather(packed, 'seq', axis=0, tiled=False)  47.4 us
    all_to_all x1, waiting for transfers between devices, per_device(): recv = lax.all_to_all(send, 'seq', 0, 0, tiled=True)  37 us
    all_to_all x1, starting transfers between devices, per_device(): recv = lax.all_to_all(send, 'seq', 0, 0, tiled=True)  10.5 us
    all_to_all x1, waiting for transfers between devices, per_device(): recv2 = lax.all_to_all(send2, 'seq', 0, 0, tiled=True)  9.8 us
    all_to_all x1, starting transfers between devices, per_device(): recv2 = lax.all_to_all(send2, 'seq', 0, 0, tiled=True)  5.36 us
    dot_general x1, matrix products, per_device(): jnp.einsum('tk,sck->tsc', both, gathered[:, :lead, :], preferred_element_...  5.24 us
    slice x1, local copies, waits for them, and re-layouts, per_device(): out_cross = outs_g[:, :, attn:].reshape(-1, attn)  4.62 us
    unnamed x21, local copies, waits for them, and re-layouts  4.22 us
  transfers between devices with their start and end apart: 3, of which 3 were waited for; matrix products, arithmetic and copies ran while one was open for 10% of the time, Pallas kernels for 0%

profile of v8, /device:TPU:1, one launch (start us, length us, event | category | flops | bytes accessed | tf_op | source)
XLA Modules:
  0.0 169.6 jit_solution(9205886959650580212)
XLA Ops:
  6.5 2.1 %fusion.38 = bf16[144,1152]{1,0:T(8,128)(2,1)} fusion(bf16[576,36]{0,1:T(8,128)(2,1)} %param.16, bf16[576,36]{0,1:T(8,128)(2,1)} %param.13, bf16[1152,18]{0,1:T(8,128)(2,1)} %param.14, bf16[1152,36]{0,1:T(8,128)(2,1)} %param.15, bf16[1152,54]{0,1:T(8,128)(2,1)} %param.12), kind=kOutput, calls=%fused_computation.58 | convolution fusion | flops 49455360 | bytes 663552 | tf_op jit(solution)/shard_map/rc,kc->rk/dot_general | solution.py:46
  9.7 1.1 pad_maximum_fusion
  10.8 10.5 %all-to-all-start = ((bf16[32,16,1152]{2,1,0:T(8,128)(2,1)}), bf16[32,16,1152]{2,1,0:T(8,128)(2,1)S(1)}, u32[]{:S(2)}, u32[]{:S(2)}) async-start(bf16[32,16,1152]{2,1,0:T(8,128)(2,1)} %pad_maximum_fusion), calls=%async_computation | async-start | bytes 2359296 | tf_op jit(solution)/shard_map/all_to_all | solution.py:96
  22.1 37.0 %all-to-all-done = bf16[32,16,1152]{2,1,0:T(8,128)(2,1)S(1)} async-done(((bf16[32,16,1152]{2,1,0:T(8,128)(2,1)}), bf16[32,16,1152]{2,1,0:T(8,128)(2,1)S(1)}, u32[]{:S(2)}, u32[]{:S(2)}) %all-to-all-start) | async-done | bytes 1179680 | tf_op jit(solution)/shard_map/all_to_all | solution.py:96
  59.2 47.4 %all-gather.3.cloned.1.call-done = bf16[4608,1152]{1,0:T(8,128)(2,1)} async-done(((bf16[144,1152]{1,0:T(8,128)(2,1)}), bf16[4608,1152]{1,0:T(8,128)(2,1)}) %all-gather.3.cloned.1.call-update) | async-done | bytes 10616848 | tf_op jit(solution)/shard_map/all_gather | solution.py:80
  106.6 5.2 %fusion.6 = bf16[264,32,96]{2,0,1:T(8,128)(2,1)S(1)} fusion(bf16[32,144,1152]{2,1,0:T(8,128)(2,1)} %bitcast.72, bf16[8,1152]{1,0:T(8,128)(2,1)S(1)} %dynamic-slice_bitcast_fusion, bf16[256,1152]{1,0:T(8,128)(2,1)S(1)} %get-tuple-element.10), kind=kOutput, calls=%fused_computation.12 | convolution fusion | flops 1870589952 | bytes 9308160 | tf_op jit(solution)/shard_map/tk,sck->tsc/dot_general | solution.py:104
  112.4 1.8 %copy.32 = bf16[256,32,54]{0,2,1:T(8,128)(2,1)} copy(bf16[256,32,54]{2,0,1:T(8,128)(2,1)S(1)} %slice.88) | data formatting | bytes 1769472 | tf_op jit(solution)/shard_map/slice | solution.py:108
  114.2 1.3 convert_element_type.56
  116.3 0.6 fusion.9
  117.7 0.7 reshape_reshape.6
  118.4 0.5 broadcast.158
  119.0 1.3 reduce.10
  120.3 1.1 reshape.174
  121.4 5.4 %all-to-all-start.1 = ((bf16[32,2,6912]{2,1,0:T(2,128)(2,1)}), bf16[32,2,6912]{2,1,0:T(2,128)(2,1)S(1)}, u32[]{:S(2)}, u32[]{:S(2)}) async-start(bf16[32,2,6912]{2,1,0:T(2,128)(2,1)} %reshape.174), calls=%async_computation.1 | async-start | bytes 1769472 | tf_op jit(solution)/shard_map/all_to_all | solution.py:122
  126.8 0.6 fusion.56
  127.4 0.6 iota_compare_fusion.2
  128.1 3.6 %slice.100 = bf16[32,18,1152]{2,1,0:T(8,128)(2,1)} slice(bf16[32,144,1152]{2,1,0:T(8,128)(2,1)} %bitcast.73), slice={[0:32], [90:108], [0:1152]} | slice | bytes 2654208 | tf_op jit(solution)/shard_map/slice | solution.py:84
  131.7 4.6 %fusion.63 = (bf16[32,36,576]{2,1,0:T(8,128)(2,1)}, bf16[32,36,576]{2,1,0:T(8,128)(2,1)S(1)}) fusion(bf16[32,144,1152]{2,1,0:T(8,128)(2,1)} %bitcast.74), kind=kLoop, calls=%fused_computation.98 | loop fusion | bytes 5308416 | tf_op jit(solution)/shard_map/slice | solution.py:127
  136.3 3.5 %reshape.161 = bf16[1152,576]{1,0:T(8,128)(2,1)} reshape(bf16[32,36,576]{2,1,0:T(8,128)(2,1)} %get-tuple-element.8) | data formatting | bytes 2654208 | tf_op jit(solution)/shard_map/reshape | solution.py:127
  139.8 1.5 reshape.156
  141.4 9.8 %all-to-all-done.1 = bf16[32,2,6912]{2,1,0:T(2,128)(2,1)S(1)} async-done(((bf16[32,2,6912]{2,1,0:T(2,128)(2,1)}), bf16[32,2,6912]{2,1,0:T(2,128)(2,1)S(1)}, u32[]{:S(2)}, u32[]{:S(2)}) %all-to-all-start.1) | async-done | bytes 884768 | tf_op jit(solution)/shard_map/all_to_all | solution.py:122
  151.2 0.7 reshape.175
  152.6 0.8 fusion.65
  153.5 1.9 %copy.38 = bf16[256,576]{0,1:T(8,128)(2,1)} copy(bf16[256,576]{1,0:T(8,128)(2,1)} %get-tuple-element.15) | data formatting | bytes 589824 | tf_op jit(solution)/shard_map/slice | solution.py:131
  155.3 0.9 copy.37
  156.2 0.7 fusion.4
  156.9 0.8 copy-done.3
  157.7 0.6 multiply_reduce_fusion
  159.2 0.7 bitcast_reduce_fusion
  159.9 0.5 fusion.18
  160.4 0.9 copy-done.1
  161.3 1.5 fusion.5
  (60 shorter events, 5.0 us)
Async XLA Ops:
  6.5 2.1 %copy-start.7 = (f32[3,1152]{1,0:T(4,128)S(1)}, f32[3,1152]{1,0:T(4,128)}, u32[]{:S(2)}) copy-start(f32[3,1152]{1,0:T(4,128)} %param.11) | copy-start | bytes 41476
  6.5 2.2 %copy-start = (bf16[1,256,1152]{2,1,0:T(8,128)(2,1)S(1)}, bf16[1,256,1152]{2,1,0:T(8,128)(2,1)}, u32[]{:S(2)}) copy-start(bf16[1,256,1152]{2,1,0:T(8,128)(2,1)} %param.10) | copy-start | bytes 1769476
  6.5 100.0 %all-gather.3.cloned.1.call-start = ((), (), s32[]{:S(2)}) async-start(), calls=%async_computation.2 | async-start | bytes 10948608 | tf_op jit(solution)/shard_map/all_gather | solution.py:80
  8.6 1.1 copy-start.5
  10.8 48.2 %all-to-all-start = ((bf16[32,16,1152]{2,1,0:T(8,128)(2,1)}), bf16[32,16,1152]{2,1,0:T(8,128)(2,1)S(1)}, u32[]{:S(2)}, u32[]{:S(2)}) async-start(bf16[32,16,1152]{2,1,0:T(8,128)(2,1)} %pad_maximum_fusion), calls=%async_computation | async-start | bytes 2359296 | tf_op jit(solution)/shard_map/all_to_all | solution.py:96
  120.3 6.5 %copy-start.8 = (s32[32]{0:T(128)S(1)}, s32[32]{0:T(128)}, u32[]{:S(2)}) copy-start(s32[32]{0:T(128)} %param.19) | copy-start | bytes 388
  121.4 29.8 %all-to-all-start.1 = ((bf16[32,2,6912]{2,1,0:T(2,128)(2,1)}), bf16[32,2,6912]{2,1,0:T(2,128)(2,1)S(1)}, u32[]{:S(2)}, u32[]{:S(2)}) async-start(bf16[32,2,6912]{2,1,0:T(2,128)(2,1)} %reshape.174), calls=%async_computation.1 | async-start | bytes 1769472 | tf_op jit(solution)/shard_map/all_to_all | solution.py:122
  152.3 3.9 %copy-start.2 = (bf16[1152,576]{1,0:T(8,128)(2,1)S(1)}, bf16[1152,576]{1,0:T(8,128)(2,1)}, u32[]{:S(2)}) copy-start(bf16[1152,576]{1,0:T(8,128)(2,1)} %reshape.156) | copy-start | bytes 3981316
  156.2 1.5 copy-start.3
  158.3 1.0 copy-start.4
  158.8 1.1 copy-start.6
  159.9 1.4 copy-start.1
Sparse Core Ops, SparseCore 0:
  9.5 97.0 all-gather.2

commit v9 on v8

--- a/solution.py
+++ b/solution.py
@@ -112,16 +112,17 @@
     key_rows = head_norm(keyval_rows[:, :attn].astype(jnp.float32), heads).astype(jnp.bfloat16)
     kv_rows = jnp.concatenate([key_rows.reshape(txt_dev, attn), keyval_rows[:, attn:]], axis=1)
 
+    blocks = kv_rows.size // (pix_dev * attn)
     send2 = jnp.concatenate(
         [
-            attended.reshape(count, -1),
-            jnp.broadcast_to(kv_rows.reshape(1, -1), (count, txt_dev * 2 * attn)),
+            attended.reshape(count, 1, pix_dev * attn),
+            jnp.broadcast_to(kv_rows.reshape(1, blocks, pix_dev * attn), (count, blocks, pix_dev * attn)),
         ],
         axis=1,
     )
     recv2 = lax.all_to_all(send2, "seq", 0, 0, tiled=True)
-    returned = recv2[:, : pix_dev * attn].reshape(pixels, attn)
-    keyval = recv2[:, pix_dev * attn :].reshape(text_len, 2 * attn)
+    returned = recv2[:, 0, :].reshape(pixels, attn)
+    keyval = recv2[:, 1:, :].reshape(text_len, 2 * attn)
 
     out_self = outs_g[:, :, :attn].reshape(-1, attn)
     out_cross = outs_g[:, :, attn:].reshape(-1, attn)

time: 170 us -> 178 us (1.047)
  waiting for transfers between devices: 94.2 us -> 100 us
    all_to_all x1, waiting for transfers between devices: 9.8 us -> 16 us  [per_device(): recv2 = lax.all_to_all(send2, 'seq', 0, 0, tiled=True)]
    concatenate x0 -> x1, other arithmetic: none -> 2.31 us  [per_device(): jnp.concatenate([attended.reshape(count, 1, pix_dev * attn), jnp.broadcas...]
    slice x2, local copies, waits for them, and re-layouts: 0.06 us -> 2.2 us  [the longest x1 1.57 us: per_device(): returned = recv2[:, 0, :].reshape(pixels, attn)]
    unnamed x21 -> x18, local copies, waits for them, and re-layouts: 4.22 us -> 2.64 us
  transfers between devices with their start and end apart: 3 -> 3, of which waited for: 3 -> 3; matrix products, arithmetic and copies ran while one was open for 10% -> 9% of each run, Pallas kernels for 0% -> 0%
where the time goes in v9:
time: 178 us; the launch traced here: 177 us
  waiting for transfers between devices  100 us (56%)
  local copies, waits for them, and re-layouts  28.3 us (16%)
  starting transfers between devices  16 us (9%)
  between operations  14.4 us (8%)
  matrix products  12.3 us (7%)
  other arithmetic  6.03 us (3%)
    all_gather x1, waiting for transfers between devices, per_device(): gathered = lax.all_gather(packed, 'seq', axis=0, tiled=False)  47.4 us
    all_to_all x1, waiting for transfers between devices, per_device(): recv = lax.all_to_all(send, 'seq', 0, 0, tiled=True)  37 us
    all_to_all x1, waiting for transfers between devices, per_device(): recv2 = lax.all_to_all(send2, 'seq', 0, 0, tiled=True)  16 us
    all_to_all x1, starting transfers between devices, per_device(): recv = lax.all_to_all(send, 'seq', 0, 0, tiled=True)  10.5 us
    all_to_all x1, starting transfers between devices, per_device(): recv2 = lax.all_to_all(send2, 'seq', 0, 0, tiled=True)  5.49 us
    dot_general x1, matrix products, per_device(): jnp.einsum('tk,sck->tsc', both, gathered[:, :lead, :], preferred_element_...  5.24 us
    slice x1, local copies, waits for them, and re-layouts, per_device(): out_cross = outs_g[:, :, attn:].reshape(-1, attn)  4.62 us
    slice x1, local copies, waits for them, and re-layouts, per_device(): query_g = gathered[:, q_at:q_at + sizes[2], :]  3.61 us
  transfers between devices with their start and end apart: 3, of which 3 were waited for; matrix products, arithmetic and copies ran while one was open for 9% of the time, Pallas kernels for 0%

profile of v9, /device:TPU:1, one launch (start us, length us, event | category | flops | bytes accessed | tf_op | source)
XLA Modules:
  0.0 177.4 jit_solution(10662789980460813037)
XLA Ops:
  6.5 2.1 %fusion.38 = bf16[144,1152]{1,0:T(8,128)(2,1)} fusion(bf16[576,36]{0,1:T(8,128)(2,1)} %param.16, bf16[576,36]{0,1:T(8,128)(2,1)} %param.13, bf16[1152,18]{0,1:T(8,128)(2,1)} %param.14, bf16[1152,36]{0,1:T(8,128)(2,1)} %param.15, bf16[1152,54]{0,1:T(8,128)(2,1)} %param.12), kind=kOutput, calls=%fused_computation.58 | convolution fusion | flops 49455360 | bytes 663552 | tf_op jit(solution)/shard_map/rc,kc->rk/dot_general | solution.py:46
  9.7 1.1 pad_maximum_fusion
  10.8 10.5 %all-to-all-start = ((bf16[32,16,1152]{2,1,0:T(8,128)(2,1)}), bf16[32,16,1152]{2,1,0:T(8,128)(2,1)S(1)}, u32[]{:S(2)}, u32[]{:S(2)}) async-start(bf16[32,16,1152]{2,1,0:T(8,128)(2,1)} %pad_maximum_fusion), calls=%async_computation | async-start | bytes 2359296 | tf_op jit(solution)/shard_map/all_to_all | solution.py:96
  22.1 37.0 %all-to-all-done = bf16[32,16,1152]{2,1,0:T(8,128)(2,1)S(1)} async-done(((bf16[32,16,1152]{2,1,0:T(8,128)(2,1)}), bf16[32,16,1152]{2,1,0:T(8,128)(2,1)S(1)}, u32[]{:S(2)}, u32[]{:S(2)}) %all-to-all-start) | async-done | bytes 1179680 | tf_op jit(solution)/shard_map/all_to_all | solution.py:96
  59.2 47.4 %all-gather.3.cloned.1.call-done = bf16[4608,1152]{1,0:T(8,128)(2,1)} async-done(((bf16[144,1152]{1,0:T(8,128)(2,1)}), bf16[4608,1152]{1,0:T(8,128)(2,1)}) %all-gather.3.cloned.1.call-update) | async-done | bytes 10616848 | tf_op jit(solution)/shard_map/all_gather | solution.py:80
  106.6 5.2 %fusion.6 = bf16[264,32,96]{2,0,1:T(8,128)(2,1)S(1)} fusion(bf16[32,144,1152]{2,1,0:T(8,128)(2,1)} %bitcast.65, bf16[8,1152]{1,0:T(8,128)(2,1)S(1)} %dynamic-slice_bitcast_fusion, bf16[256,1152]{1,0:T(8,128)(2,1)S(1)} %get-tuple-element.10), kind=kOutput, calls=%fused_computation.12 | convolution fusion | flops 1870589952 | bytes 9308160 | tf_op jit(solution)/shard_map/tk,sck->tsc/dot_general | solution.py:104
  112.4 1.8 copy.14
  114.2 1.3 convert_element_type.56
  116.2 0.6 fusion.9
  116.8 0.5 fusion.17
  117.6 1.0 reshape_reshape.8
  118.9 2.3 %pad_maximum_fusion.1 = bf16[32,3,4608]{2,1,0:T(4,128)(2,1)} fusion(bf16[32,2,4608]{2,1,0:T(2,128)(2,1)S(1)} %broadcast_in_dim.39, bf16[32,1,4608]{2,1,0:T(2,128)(2,1)S(1)} %reshape_reshape.8), kind=kLoop, calls=%fused_computation.33 | loop fusion | flops 1769472 | bytes 1769472 | tf_op jit(solution)/shard_map/concatenate | solution.py:116
  121.3 5.5 %all-to-all-start.1 = ((bf16[32,3,4608]{2,1,0:T(4,128)(2,1)}), bf16[32,3,4608]{2,1,0:T(4,128)(2,1)S(1)}, u32[]{:S(2)}, u32[]{:S(2)}) async-start(bf16[32,3,4608]{2,1,0:T(4,128)(2,1)} %pad_maximum_fusion.1), calls=%async_computation.1 | async-start | bytes 2359296 | tf_op jit(solution)/shard_map/all_to_all | solution.py:123
  126.8 0.6 fusion.56
  127.4 0.6 iota_compare_fusion.2
  128.1 3.6 %slice.100 = bf16[32,18,1152]{2,1,0:T(8,128)(2,1)} slice(bf16[32,144,1152]{2,1,0:T(8,128)(2,1)} %bitcast.66), slice={[0:32], [90:108], [0:1152]} | slice | bytes 2654208 | tf_op jit(solution)/shard_map/slice | solution.py:84
  131.7 4.6 %fusion.63 = (bf16[32,36,576]{2,1,0:T(8,128)(2,1)}, bf16[32,36,576]{2,1,0:T(8,128)(2,1)S(1)}) fusion(bf16[32,144,1152]{2,1,0:T(8,128)(2,1)} %bitcast.67), kind=kLoop, calls=%fused_computation.98 | loop fusion | bytes 5308416 | tf_op jit(solution)/shard_map/slice | solution.py:128
  136.3 3.5 %reshape.155 = bf16[1152,576]{1,0:T(8,128)(2,1)} reshape(bf16[32,36,576]{2,1,0:T(8,128)(2,1)} %get-tuple-element.8) | data formatting | bytes 2654208 | tf_op jit(solution)/shard_map/reshape | solution.py:128
  139.8 1.5 reshape.150
  141.4 16.0 %all-to-all-done.1 = bf16[32,3,4608]{2,1,0:T(4,128)(2,1)S(1)} async-done(((bf16[32,3,4608]{2,1,0:T(4,128)(2,1)}), bf16[32,3,4608]{2,1,0:T(4,128)(2,1)S(1)}, u32[]{:S(2)}, u32[]{:S(2)}) %all-to-all-start.1) | async-done | bytes 884768 | tf_op jit(solution)/shard_map/all_to_all | solution.py:123
  157.4 0.6 slice.97
  158.2 1.6 slice_reduce_fusion
  160.0 0.8 fusion.65
  160.9 1.9 %copy.20 = bf16[256,576]{0,1:T(8,128)(2,1)} copy(bf16[256,576]{1,0:T(8,128)(2,1)} %get-tuple-element.15) | data formatting | bytes 589824 | tf_op jit(solution)/shard_map/slice | solution.py:132
  162.7 0.9 copy.19
  163.6 0.7 fusion.4
  164.3 0.8 copy-done.3
  165.1 0.6 multiply_reduce_fusion
  166.6 0.7 bitcast_reduce_fusion
  167.6 0.5 fusion.18
  168.1 0.9 copy-done.1
  169.0 1.5 fusion.5
  (55 shorter events, 4.7 us)
Async XLA Ops:
  6.5 2.1 %copy-start.7 = (f32[3,1152]{1,0:T(4,128)S(1)}, f32[3,1152]{1,0:T(4,128)}, u32[]{:S(2)}) copy-start(f32[3,1152]{1,0:T(4,128)} %param.11) | copy-start | bytes 41476
  6.5 2.2 %copy-start = (bf16[1,256,1152]{2,1,0:T(8,128)(2,1)S(1)}, bf16[1,256,1152]{2,1,0:T(8,128)(2,1)}, u32[]{:S(2)}) copy-start(bf16[1,256,1152]{2,1,0:T(8,128)(2,1)} %param.10) | copy-start | bytes 1769476
  6.5 100.0 %all-gather.3.cloned.1.call-start = ((), (), s32[]{:S(2)}) async-start(), calls=%async_computation.2 | async-start | bytes 10948608 | tf_op jit(solution)/shard_map/all_gather | solution.py:80
  8.6 1.1 copy-start.5
  10.8 48.2 %all-to-all-start = ((bf16[32,16,1152]{2,1,0:T(8,128)(2,1)}), bf16[32,16,1152]{2,1,0:T(8,128)(2,1)S(1)}, u32[]{:S(2)}, u32[]{:S(2)}) async-start(bf16[32,16,1152]{2,1,0:T(8,128)(2,1)} %pad_maximum_fusion), calls=%async_computation | async-start | bytes 2359296 | tf_op jit(solution)/shard_map/all_to_all | solution.py:96
  121.3 5.5 %copy-start.8 = (s32[32]{0:T(128)S(1)}, s32[32]{0:T(128)}, u32[]{:S(2)}) copy-start(s32[32]{0:T(128)} %param.19) | copy-start | bytes 388
  121.3 36.1 %all-to-all-start.1 = ((bf16[32,3,4608]{2,1,0:T(4,128)(2,1)}), bf16[32,3,4608]{2,1,0:T(4,128)(2,1)S(1)}, u32[]{:S(2)}, u32[]{:S(2)}) async-start(bf16[32,3,4608]{2,1,0:T(4,128)(2,1)} %pad_maximum_fusion.1), calls=%async_computation.1 | async-start | bytes 2359296 | tf_op jit(solution)/shard_map/all_to_all | solution.py:123
  159.8 3.9 %copy-start.2 = (bf16[1152,576]{1,0:T(8,128)(2,1)S(1)}, bf16[1152,576]{1,0:T(8,128)(2,1)}, u32[]{:S(2)}) copy-start(bf16[1152,576]{1,0:T(8,128)(2,1)} %reshape.150) | copy-start | bytes 3981316
  163.6 1.5 copy-start.3
  165.7 1.0 copy-start.4
  166.6 1.0 copy-start.6
  167.6 1.4 copy-start.1
Sparse Core Ops, SparseCore 0:
  9.5 97.0 all-gather.2

commit v10 on v8

--- a/solution.py
+++ b/solution.py
@@ -99,16 +99,20 @@
     memory_rows = lax.dynamic_index_in_dim(recv[:, pix_dev:, :], pick, 0, keepdims=False)
 
     flat_pix = switched.reshape(-1, width)
-    both = jnp.concatenate([flat_pix, memory_rows], axis=0)
-    lead = -(-(kv_at + sizes[1]) // 16) * 16
-    both_out = jnp.einsum(
-        "tk,sck->tsc", both, gathered[:, :lead, :], preferred_element_type=jnp.float32
+    q_end = -(-sizes[0] // 16) * 16
+    qkv_out = jnp.einsum(
+        "tk,sck->tsc", flat_pix, gathered[:, :q_end, :], preferred_element_type=jnp.float32
     )
     tok = flat_pix.shape[0]
-    qkv = both_out[:tok, :, : sizes[0]].reshape(tok, -1).astype(jnp.bfloat16)
+    qkv = qkv_out[:, :, : sizes[0]].reshape(tok, -1).astype(jnp.bfloat16)
     attended = temporal_attention(qkv, heads, attn, scale_q, pix_dev)
 
-    keyval_rows = both_out[tok:, :, kv_at : kv_at + sizes[1]].reshape(txt_dev, -1).astype(jnp.bfloat16)
+    kv_lo = kv_at // 16 * 16
+    kv_hi = -(-(kv_at + sizes[1]) // 16) * 16
+    kv_out = jnp.einsum(
+        "tk,sck->tsc", memory_rows, gathered[:, kv_lo:kv_hi, :], preferred_element_type=jnp.float32
+    )
+    keyval_rows = kv_out[:, :, kv_at - kv_lo : kv_at - kv_lo + sizes[1]].reshape(txt_dev, -1).astype(jnp.bfloat16)
     key_rows = head_norm(keyval_rows[:, :attn].astype(jnp.float32), heads).astype(jnp.bfloat16)
     kv_rows = jnp.concatenate([key_rows.reshape(txt_dev, attn), keyval_rows[:, attn:]], axis=1)
 

time: 170 us -> 170 us (level)
  local copies, waits for them, and re-layouts: 27.8 us -> 24.7 us
  matrix products: 12.3 us -> 14.9 us
    dot_general x1 -> x2, matrix products: 5.24 us -> 7.85 us  [the longest x1 3.94 us: per_device(): jnp.einsum('tk,sck->tsc', memory_rows, gathered[:, kv_lo:kv_hi, :], prefe...]
    slice x4, local copies, waits for them, and re-layouts: 2.11 us -> 0.25 us  [the longest x2 0.13 us: per_device(): kv_out[:, :, kv_at - kv_lo:kv_at - kv_lo + sizes[1]].reshape(txt_dev, -1)]
where the time goes in v10:
time: 170 us; the launch traced here: 169 us
  waiting for transfers between devices  94.3 us (55%)
  local copies, waits for them, and re-layouts  24.7 us (15%)
  starting transfers between devices  15.8 us (9%)
  matrix products  14.9 us (9%)
  between operations  14.4 us (8%)
  other arithmetic  5.12 us (3%)
    all_gather x1, waiting for transfers between devices, per_device(): gathered = lax.all_gather(packed, 'seq', axis=0, tiled=False)  47.4 us
    all_to_all x1, waiting for transfers between devices, per_device(): recv = lax.all_to_all(send, 'seq', 0, 0, tiled=True)  37 us
    all_to_all x1, starting transfers between devices, per_device(): recv = lax.all_to_all(send, 'seq', 0, 0, tiled=True)  10.5 us
    all_to_all x1, waiting for transfers between devices, per_device(): recv2 = lax.all_to_all(send2, 'seq', 0, 0, tiled=True)  9.8 us
    all_to_all x1, starting transfers between devices, per_device(): recv2 = lax.all_to_all(send2, 'seq', 0, 0, tiled=True)  5.37 us
    slice x1, local copies, waits for them, and re-layouts, per_device(): out_cross = outs_g[:, :, attn:].reshape(-1, attn)  4.62 us
    unnamed x21, local copies, waits for them, and re-layouts  4.22 us
    dot_general x1, matrix products, per_device(): jnp.einsum('tk,sck->tsc', memory_rows, gathered[:, kv_lo:kv_hi, :], prefe...  3.94 us
  transfers between devices with their start and end apart: 3, of which 3 were waited for; matrix products, arithmetic and copies ran while one was open for 10% of the time, Pallas kernels for 0%

profile of v10, /device:TPU:1, one launch (start us, length us, event | category | flops | bytes accessed | tf_op | source)
XLA Modules:
  0.0 169.2 jit_solution(15219114458886749729)
XLA Ops:
  6.5 2.1 %fusion.35 = bf16[144,1152]{1,0:T(8,128)(2,1)} fusion(bf16[576,36]{0,1:T(8,128)(2,1)} %param.16, bf16[576,36]{0,1:T(8,128)(2,1)} %param.13, bf16[1152,18]{0,1:T(8,128)(2,1)} %param.14, bf16[1152,36]{0,1:T(8,128)(2,1)} %param.15, bf16[1152,54]{0,1:T(8,128)(2,1)} %param.12), kind=kOutput, calls=%fused_computation.57 | convolution fusion | flops 49455360 | bytes 663552 | tf_op jit(solution)/shard_map/rc,kc->rk/dot_general | solution.py:46
  9.7 1.1 pad_maximum_fusion
  10.8 10.5 %all-to-all-start = ((bf16[32,16,1152]{2,1,0:T(8,128)(2,1)}), bf16[32,16,1152]{2,1,0:T(8,128)(2,1)S(1)}, u32[]{:S(2)}, u32[]{:S(2)}) async-start(bf16[32,16,1152]{2,1,0:T(8,128)(2,1)} %pad_maximum_fusion), calls=%async_computation | async-start | bytes 2359296 | tf_op jit(solution)/shard_map/all_to_all | solution.py:96
  22.1 37.0 %all-to-all-done = bf16[32,16,1152]{2,1,0:T(8,128)(2,1)S(1)} async-done(((bf16[32,16,1152]{2,1,0:T(8,128)(2,1)}), bf16[32,16,1152]{2,1,0:T(8,128)(2,1)S(1)}, u32[]{:S(2)}, u32[]{:S(2)}) %all-to-all-start) | async-done | bytes 1179680 | tf_op jit(solution)/shard_map/all_to_all | solution.py:96
  59.1 47.4 %all-gather.3.cloned.1.call-done = bf16[4608,1152]{1,0:T(8,128)(2,1)} async-done(((bf16[144,1152]{1,0:T(8,128)(2,1)}), bf16[4608,1152]{1,0:T(8,128)(2,1)}) %all-gather.3.cloned.1.call-update) | async-done | bytes 10616848 | tf_op jit(solution)/shard_map/all_gather | solution.py:80
  106.6 3.9 %fusion.2 = bf16[8,32,48]{2,0,1:T(8,128)(2,1)S(1)} fusion(bf16[32,144,1152]{2,1,0:T(8,128)(2,1)} %bitcast.74, bf16[32,8,1152]{2,1,0:T(8,128)(2,1)S(1)} %slice.95, s32[]{:T(128)S(6)} %select_n.36), kind=kOutput, calls=%fused_computation.2 | convolution fusion | flops 28311552 | bytes 3581956 | tf_op jit(solution)/shard_map/tk,sck->tsc/dot_general | solution.py:112
  110.9 3.9 %fusion = bf16[256,32,64]{0,2,1:T(8,128)(2,1)S(1)} fusion(bf16[32,144,1152]{2,1,0:T(8,128)(2,1)} %bitcast.75, bf16[32,16,1152]{2,1,0:T(8,128)(2,1)S(1)} %all-to-all-done), kind=kOutput, calls=%fused_computation | convolution fusion | flops 1207959552 | bytes 6356992 | tf_op jit(solution)/shard_map/tk,sck->tsc/dot_general | solution.py:103
  115.8 0.6 fusion.8
  116.5 0.5 fusion.16
  117.3 0.7 reshape_reshape.6
  118.0 0.5 broadcast.158
  118.6 1.3 reduce.10
  119.9 1.1 reshape.175
  121.0 5.4 %all-to-all-start.1 = ((bf16[32,2,6912]{2,1,0:T(2,128)(2,1)}), bf16[32,2,6912]{2,1,0:T(2,128)(2,1)S(1)}, u32[]{:S(2)}, u32[]{:S(2)}) async-start(bf16[32,2,6912]{2,1,0:T(2,128)(2,1)} %reshape.175), calls=%async_computation.1 | async-start | bytes 1769472 | tf_op jit(solution)/shard_map/all_to_all | solution.py:126
  126.4 0.6 fusion.55
  127.0 0.6 iota_compare_fusion.2
  127.7 3.6 %slice.105 = bf16[32,18,1152]{2,1,0:T(8,128)(2,1)} slice(bf16[32,144,1152]{2,1,0:T(8,128)(2,1)} %bitcast.76), slice={[0:32], [90:108], [0:1152]} | slice | bytes 2654208 | tf_op jit(solution)/shard_map/slice | solution.py:84
  131.3 4.6 %fusion.62 = (bf16[32,36,576]{2,1,0:T(8,128)(2,1)}, bf16[32,36,576]{2,1,0:T(8,128)(2,1)S(1)}) fusion(bf16[32,144,1152]{2,1,0:T(8,128)(2,1)} %bitcast.77), kind=kLoop, calls=%fused_computation.99 | loop fusion | bytes 5308416 | tf_op jit(solution)/shard_map/slice | solution.py:131
  135.9 3.5 %reshape.161 = bf16[1152,576]{1,0:T(8,128)(2,1)} reshape(bf16[32,36,576]{2,1,0:T(8,128)(2,1)} %get-tuple-element.8) | data formatting | bytes 2654208 | tf_op jit(solution)/shard_map/reshape | solution.py:131
  139.4 1.5 reshape.156
  141.0 9.8 %all-to-all-done.1 = bf16[32,2,6912]{2,1,0:T(2,128)(2,1)S(1)} async-done(((bf16[32,2,6912]{2,1,0:T(2,128)(2,1)}), bf16[32,2,6912]{2,1,0:T(2,128)(2,1)S(1)}, u32[]{:S(2)}, u32[]{:S(2)}) %all-to-all-start.1) | async-done | bytes 884768 | tf_op jit(solution)/shard_map/all_to_all | solution.py:126
  150.8 0.7 reshape.176
  152.2 0.8 fusion.64
  153.1 1.9 %copy.35 = bf16[256,576]{0,1:T(8,128)(2,1)} copy(bf16[256,576]{1,0:T(8,128)(2,1)} %get-tuple-element.13) | data formatting | bytes 589824 | tf_op jit(solution)/shard_map/slice | solution.py:135
  154.9 0.9 copy.34
  155.8 0.7 fusion.6
  156.5 0.8 copy-done.3
  157.3 0.6 multiply_reduce_fusion
  158.8 0.7 bitcast_reduce_fusion
  159.5 0.5 fusion.17
  160.0 0.9 copy-done.1
  160.9 1.5 fusion.7
  (59 shorter events, 4.6 us)
Async XLA Ops:
  6.5 2.1 %copy-start.7 = (f32[3,1152]{1,0:T(4,128)S(1)}, f32[3,1152]{1,0:T(4,128)}, u32[]{:S(2)}) copy-start(f32[3,1152]{1,0:T(4,128)} %param.11) | copy-start | bytes 41476
  6.5 2.2 %copy-start = (bf16[1,256,1152]{2,1,0:T(8,128)(2,1)S(1)}, bf16[1,256,1152]{2,1,0:T(8,128)(2,1)}, u32[]{:S(2)}) copy-start(bf16[1,256,1152]{2,1,0:T(8,128)(2,1)} %param.10) | copy-start | bytes 1769476
  6.5 100.0 %all-gather.3.cloned.1.call-start = ((), (), s32[]{:S(2)}) async-start(), calls=%async_computation.2 | async-start | bytes 10948608 | tf_op jit(solution)/shard_map/all_gather | solution.py:80
  8.6 1.1 copy-start.5
  10.8 48.2 %all-to-all-start = ((bf16[32,16,1152]{2,1,0:T(8,128)(2,1)}), bf16[32,16,1152]{2,1,0:T(8,128)(2,1)S(1)}, u32[]{:S(2)}, u32[]{:S(2)}) async-start(bf16[32,16,1152]{2,1,0:T(8,128)(2,1)} %pad_maximum_fusion), calls=%async_computation | async-start | bytes 2359296 | tf_op jit(solution)/shard_map/all_to_all | solution.py:96
  119.9 6.5 %copy-start.8 = (s32[32]{0:T(128)S(1)}, s32[32]{0:T(128)}, u32[]{:S(2)}) copy-start(s32[32]{0:T(128)} %param.19) | copy-start | bytes 388
  121.0 29.8 %all-to-all-start.1 = ((bf16[32,2,6912]{2,1,0:T(2,128)(2,1)}), bf16[32,2,6912]{2,1,0:T(2,128)(2,1)S(1)}, u32[]{:S(2)}, u32[]{:S(2)}) async-start(bf16[32,2,6912]{2,1,0:T(2,128)(2,1)} %reshape.175), calls=%async_computation.1 | async-start | bytes 1769472 | tf_op jit(solution)/shard_map/all_to_all | solution.py:126
  151.9 3.9 %copy-start.2 = (bf16[1152,576]{1,0:T(8,128)(2,1)S(1)}, bf16[1152,576]{1,0:T(8,128)(2,1)}, u32[]{:S(2)}) copy-start(bf16[1152,576]{1,0:T(8,128)(2,1)} %reshape.156) | copy-start | bytes 3981316
  155.8 1.5 copy-start.3
  157.9 1.0 copy-start.4
  158.4 1.1 copy-start.6
  159.5 1.4 copy-start.1
Sparse Core Ops, SparseCore 0:
  9.5 97.0 all-gather.2

commit v11 on v10

--- a/solution.py
+++ b/solution.py
@@ -110,9 +110,10 @@
     kv_lo = kv_at // 16 * 16
     kv_hi = -(-(kv_at + sizes[1]) // 16) * 16
     kv_out = jnp.einsum(
-        "tk,sck->tsc", memory_rows, gathered[:, kv_lo:kv_hi, :], preferred_element_type=jnp.float32
+        "sck,tk->sct", gathered[:, kv_lo:kv_hi, :], memory_rows, preferred_element_type=jnp.float32
     )
-    keyval_rows = kv_out[:, :, kv_at - kv_lo : kv_at - kv_lo + sizes[1]].reshape(txt_dev, -1).astype(jnp.bfloat16)
+    kv_out = kv_out[:, kv_at - kv_lo : kv_at - kv_lo + sizes[1], :].astype(jnp.bfloat16)
+    keyval_rows = jnp.transpose(kv_out, (2, 0, 1)).reshape(txt_dev, -1)
     key_rows = head_norm(keyval_rows[:, :attn].astype(jnp.float32), heads).astype(jnp.bfloat16)
     kv_rows = jnp.concatenate([key_rows.reshape(txt_dev, attn), keyval_rows[:, attn:]], axis=1)
 

time: 170 us -> 170 us (level)
  no operation moved by 1% of the time
where the time goes in v11:
time: 170 us; the launch traced here: 169 us
  waiting for transfers between devices  94.3 us (55%)
  local copies, waits for them, and re-layouts  24.7 us (15%)
  starting transfers between devices  15.8 us (9%)
  matrix products  14.9 us (9%)
  between operations  14.4 us (8%)
  other arithmetic  5.12 us (3%)
    all_gather x1, waiting for transfers between devices, per_device(): gathered = lax.all_gather(packed, 'seq', axis=0, tiled=False)  47.4 us
    all_to_all x1, waiting for transfers between devices, per_device(): recv = lax.all_to_all(send, 'seq', 0, 0, tiled=True)  37 us
    all_to_all x1, starting transfers between devices, per_device(): recv = lax.all_to_all(send, 'seq', 0, 0, tiled=True)  10.5 us
    all_to_all x1, waiting for transfers between devices, per_device(): recv2 = lax.all_to_all(send2, 'seq', 0, 0, tiled=True)  9.8 us
    all_to_all x1, starting transfers between devices, per_device(): recv2 = lax.all_to_all(send2, 'seq', 0, 0, tiled=True)  5.37 us
    slice x1, local copies, waits for them, and re-layouts, per_device(): out_cross = outs_g[:, :, attn:].reshape(-1, attn)  4.62 us
    unnamed x21, local copies, waits for them, and re-layouts  4.22 us
    dot_general x1, matrix products, per_device(): jnp.einsum('sck,tk->sct', gathered[:, kv_lo:kv_hi, :], memory_rows, prefe...  3.94 us
  transfers between devices with their start and end apart: 3, of which 3 were waited for; matrix products, arithmetic and copies ran while one was open for 10% of the time, Pallas kernels for 0%

profile of v11, /device:TPU:1, one launch (start us, length us, event | category | flops | bytes accessed | tf_op | source)
XLA Modules:
  0.0 169.2 jit_solution(7707601971286002652)
XLA Ops:
  6.5 2.1 %fusion.35 = bf16[144,1152]{1,0:T(8,128)(2,1)} fusion(bf16[576,36]{0,1:T(8,128)(2,1)} %param.16, bf16[576,36]{0,1:T(8,128)(2,1)} %param.13, bf16[1152,18]{0,1:T(8,128)(2,1)} %param.14, bf16[1152,36]{0,1:T(8,128)(2,1)} %param.15, bf16[1152,54]{0,1:T(8,128)(2,1)} %param.12), kind=kOutput, calls=%fused_computation.57 | convolution fusion | flops 49455360 | bytes 663552 | tf_op jit(solution)/shard_map/rc,kc->rk/dot_general | solution.py:46
  9.7 1.1 pad_maximum_fusion
  10.8 10.5 %all-to-all-start = ((bf16[32,16,1152]{2,1,0:T(8,128)(2,1)}), bf16[32,16,1152]{2,1,0:T(8,128)(2,1)S(1)}, u32[]{:S(2)}, u32[]{:S(2)}) async-start(bf16[32,16,1152]{2,1,0:T(8,128)(2,1)} %pad_maximum_fusion), calls=%async_computation | async-start | bytes 2359296 | tf_op jit(solution)/shard_map/all_to_all | solution.py:96
  22.1 37.0 %all-to-all-done = bf16[32,16,1152]{2,1,0:T(8,128)(2,1)S(1)} async-done(((bf16[32,16,1152]{2,1,0:T(8,128)(2,1)}), bf16[32,16,1152]{2,1,0:T(8,128)(2,1)S(1)}, u32[]{:S(2)}, u32[]{:S(2)}) %all-to-all-start) | async-done | bytes 1179680 | tf_op jit(solution)/shard_map/all_to_all | solution.py:96
  59.1 47.4 %all-gather.3.cloned.1.call-done = bf16[4608,1152]{1,0:T(8,128)(2,1)} async-done(((bf16[144,1152]{1,0:T(8,128)(2,1)}), bf16[4608,1152]{1,0:T(8,128)(2,1)}) %all-gather.3.cloned.1.call-update) | async-done | bytes 10616848 | tf_op jit(solution)/shard_map/all_gather | solution.py:80
  106.6 3.9 %fusion.2 = bf16[32,48,8]{1,2,0:T(8,128)(2,1)S(1)} fusion(bf16[32,144,1152]{2,1,0:T(8,128)(2,1)} %bitcast.76, bf16[32,8,1152]{2,1,0:T(8,128)(2,1)S(1)} %slice.96, s32[]{:T(128)S(6)} %select_n.36), kind=kOutput, calls=%fused_computation.2 | convolution fusion | flops 28311552 | bytes 3581956 | tf_op jit(solution)/shard_map/sck,tk->sct/dot_general | solution.py:112
  110.9 3.9 %fusion = bf16[256,32,64]{0,2,1:T(8,128)(2,1)S(1)} fusion(bf16[32,144,1152]{2,1,0:T(8,128)(2,1)} %bitcast.77, bf16[32,16,1152]{2,1,0:T(8,128)(2,1)S(1)} %all-to-all-done), kind=kOutput, calls=%fused_computation | convolution fusion | flops 1207959552 | bytes 6356992 | tf_op jit(solution)/shard_map/tk,sck->tsc/dot_general | solution.py:103
  115.8 0.6 fusion.8
  116.5 0.5 fusion.16
  117.3 0.7 reshape_reshape.6
  118.0 0.5 broadcast.158
  118.6 1.3 reduce.10
  119.9 1.1 reshape.177
  121.0 5.4 %all-to-all-start.1 = ((bf16[32,2,6912]{2,1,0:T(2,128)(2,1)}), bf16[32,2,6912]{2,1,0:T(2,128)(2,1)S(1)}, u32[]{:S(2)}, u32[]{:S(2)}) async-start(bf16[32,2,6912]{2,1,0:T(2,128)(2,1)} %reshape.177), calls=%async_computation.1 | async-start | bytes 1769472 | tf_op jit(solution)/shard_map/all_to_all | solution.py:127
  126.4 0.6 fusion.56
  127.0 0.6 iota_compare_fusion.2
  127.7 3.6 %slice.105 = bf16[32,18,1152]{2,1,0:T(8,128)(2,1)} slice(bf16[32,144,1152]{2,1,0:T(8,128)(2,1)} %bitcast.78), slice={[0:32], [90:108], [0:1152]} | slice | bytes 2654208 | tf_op jit(solution)/shard_map/slice | solution.py:84
  131.3 4.6 %fusion.63 = (bf16[32,36,576]{2,1,0:T(8,128)(2,1)}, bf16[32,36,576]{2,1,0:T(8,128)(2,1)S(1)}) fusion(bf16[32,144,1152]{2,1,0:T(8,128)(2,1)} %bitcast.79), kind=kLoop, calls=%fused_computation.100 | loop fusion | bytes 5308416 | tf_op jit(solution)/shard_map/slice | solution.py:132
  135.9 3.5 %reshape.163 = bf16[1152,576]{1,0:T(8,128)(2,1)} reshape(bf16[32,36,576]{2,1,0:T(8,128)(2,1)} %get-tuple-element.8) | data formatting | bytes 2654208 | tf_op jit(solution)/shard_map/reshape | solution.py:132
  139.4 1.5 reshape.158
  141.0 9.8 %all-to-all-done.1 = bf16[32,2,6912]{2,1,0:T(2,128)(2,1)S(1)} async-done(((bf16[32,2,6912]{2,1,0:T(2,128)(2,1)}), bf16[32,2,6912]{2,1,0:T(2,128)(2,1)S(1)}, u32[]{:S(2)}, u32[]{:S(2)}) %all-to-all-start.1) | async-done | bytes 884768 | tf_op jit(solution)/shard_map/all_to_all | solution.py:127
  150.8 0.7 reshape.178
  152.2 0.8 fusion.65
  153.1 1.9 %copy.35 = bf16[256,576]{0,1:T(8,128)(2,1)} copy(bf16[256,576]{1,0:T(8,128)(2,1)} %get-tuple-element.13) | data formatting | bytes 589824 | tf_op jit(solution)/shard_map/slice | solution.py:136
  154.9 0.9 copy.34
  155.8 0.7 fusion.6
  156.5 0.8 copy-done.3
  157.3 0.6 multiply_reduce_fusion
  158.8 0.7 bitcast_reduce_fusion
  159.5 0.5 fusion.17
  160.0 0.9 copy-done.1
  160.9 1.5 fusion.7
  (59 shorter events, 4.6 us)
Async XLA Ops:
  6.5 2.1 %copy-start.7 = (f32[3,1152]{1,0:T(4,128)S(1)}, f32[3,1152]{1,0:T(4,128)}, u32[]{:S(2)}) copy-start(f32[3,1152]{1,0:T(4,128)} %param.11) | copy-start | bytes 41476
  6.5 2.2 %copy-start = (bf16[1,256,1152]{2,1,0:T(8,128)(2,1)S(1)}, bf16[1,256,1152]{2,1,0:T(8,128)(2,1)}, u32[]{:S(2)}) copy-start(bf16[1,256,1152]{2,1,0:T(8,128)(2,1)} %param.10) | copy-start | bytes 1769476
  6.5 100.0 %all-gather.3.cloned.1.call-start = ((), (), s32[]{:S(2)}) async-start(), calls=%async_computation.2 | async-start | bytes 10948608 | tf_op jit(solution)/shard_map/all_gather | solution.py:80
  8.6 1.1 copy-start.5
  10.8 48.2 %all-to-all-start = ((bf16[32,16,1152]{2,1,0:T(8,128)(2,1)}), bf16[32,16,1152]{2,1,0:T(8,128)(2,1)S(1)}, u32[]{:S(2)}, u32[]{:S(2)}) async-start(bf16[32,16,1152]{2,1,0:T(8,128)(2,1)} %pad_maximum_fusion), calls=%async_computation | async-start | bytes 2359296 | tf_op jit(solution)/shard_map/all_to_all | solution.py:96
  119.9 6.5 %copy-start.8 = (s32[32]{0:T(128)S(1)}, s32[32]{0:T(128)}, u32[]{:S(2)}) copy-start(s32[32]{0:T(128)} %param.19) | copy-start | bytes 388
  121.0 29.8 %all-to-all-start.1 = ((bf16[32,2,6912]{2,1,0:T(2,128)(2,1)}), bf16[32,2,6912]{2,1,0:T(2,128)(2,1)S(1)}, u32[]{:S(2)}, u32[]{:S(2)}) async-start(bf16[32,2,6912]{2,1,0:T(2,128)(2,1)} %reshape.177), calls=%async_computation.1 | async-start | bytes 1769472 | tf_op jit(solution)/shard_map/all_to_all | solution.py:127
  151.9 3.9 %copy-start.2 = (bf16[1152,576]{1,0:T(8,128)(2,1)S(1)}, bf16[1152,576]{1,0:T(8,128)(2,1)}, u32[]{:S(2)}) copy-start(bf16[1152,576]{1,0:T(8,128)(2,1)} %reshape.158) | copy-start | bytes 3981316
  155.8 1.5 copy-start.3
  157.9 1.0 copy-start.4
  158.4 1.1 copy-start.6
  159.5 1.4 copy-start.1
Sparse Core Ops, SparseCore 0:
  9.5 97.0 all-gather.2
